TPU v7x, 768 devices: a whole 4x8x12 slice. The times are simulated.
768 devices in a mesh: island: 96 (over x, z, core), fsdp: 8 (over y).
Axes of the slice: x: 4, y: 8, z: 12, core: 2. Of those that a mesh axis runs over, the one named last changes fastest.
Arguments:
- pseudo_grad: bfloat16 [96, 8192, 512], P('island', 'fsdp'), may hold values from -40 to 40
- error_buf: bfloat16 [96, 8192, 512], P('island', 'fsdp'), may hold values from -2 to 2
- params: bfloat16 [8192, 512], P('fsdp'), may hold values from -6 to 6
- momentum: float32 [96, 1024], P('island', 'fsdp'), may hold values from -4 to 4
- sel_blocks: int32 [96, 512], P('island', 'fsdp'), may hold values from 0 to 127, as said below
- coef_index: int32 [1024, 64], P('fsdp'), may hold values from 0 to 4095, as said below
- owner_map: int32 [1024], P('fsdp'), may hold values from 0 to 95, as said below
Outputs:
- new_params: bfloat16 [8192, 512], P('fsdp')
- new_error: bfloat16 [96, 8192, 512], P('island', 'fsdp')
- new_momentum: float32 [96, 1024], P('island', 'fsdp')
Inputs may be any that keep to these rules, and one draw needn't show every extreme that they name: `sel_blocks`: each island's 64 entries for one shard are distinct blocks of that shard. `coef_index`: each row holds 64 distinct positions. `owner_map`: within each shard of 128 blocks an island owns at most 2 blocks, and some island owns exactly 2.
All inputs are finite; a program needn't handle non-finite values.
Results may differ from a plain program's by a relative error of at most 0.0032.
Values may be sent and summed in bfloat16 or wider, within the bound.
No kernel may reach another device: no remote copies, remote signals or barrier semaphores. Data moves between devices by JAX's collectives and lax.ppermute only.
A program may use at most 64 MiB of HBM per device.

v0:
```python
import jax
import jax.numpy as jnp
from jax import lax
from jax.sharding import PartitionSpec as P

BETA_FACTOR = 0.9
OUTER_RATE = 0.5
EPSILON = 1e-06
precise_mode = lax.Precision.HIGHEST


def cosine_table():
    freqs = jnp.arange(64, dtype=jnp.float32)[:, None]
    points = jnp.arange(64, dtype=jnp.float32)[None, :]
    scaling = jnp.where(freqs == 0.0, jnp.sqrt(1.0 / 64.0), jnp.sqrt(2.0 / 64.0))
    return scaling * jnp.cos(jnp.pi * (2.0 * points + 1.0) * freqs / 128.0)


def to_blocks(field):
    row_blocks = field.shape[0] // 64
    col_blocks = field.shape[1] // 64
    return (
        field.reshape(row_blocks, 64, col_blocks, 64)
        .transpose(0, 2, 1, 3)
        .reshape(row_blocks * col_blocks, 64, 64)
    )


def from_blocks(blocks, row_total, col_total):
    row_blocks = row_total // 64
    col_blocks = col_total // 64
    return (
        blocks.reshape(row_blocks, col_blocks, 64, 64)
        .transpose(0, 2, 1, 3)
        .reshape(row_total, col_total)
    )


def forward_blocks(cosine, blocks):
    return jnp.einsum("ij,bjk,lk->bil", cosine, blocks, cosine, precision=precise_mode)


def inverse_blocks(cosine, blocks):
    return jnp.einsum("ji,bjk,kl->bil", cosine, blocks, cosine, precision=precise_mode)


def scatter_coefs(values, positions):
    amount = values.shape[0]
    return (
        jnp.zeros((amount, 4096), jnp.float32)
        .at[jnp.arange(amount)[:, None], positions]
        .set(values)
    )


def on_device(pseudo_grad, error_buf, params, momentum, sel_blocks, coef_index, owner_map):
    cosine = cosine_table()
    islands = lax.axis_size("island")
    my_island = lax.axis_index("island")
    shard_rows = params.shape[0]
    columns = params.shape[1]
    n_blocks = coef_index.shape[0]
    coef_total = coef_index.shape[1]
    capacity = momentum.shape[1] // coef_total
    summed = pseudo_grad[0].astype(jnp.float32) + error_buf[0].astype(jnp.float32)
    blocks = to_blocks(summed)
    spectra = forward_blocks(cosine, blocks).reshape(n_blocks, 4096)
    picked = jnp.take_along_axis(spectra, coef_index, axis=1)
    chosen = sel_blocks[0]
    block_ids = jnp.arange(n_blocks, dtype=jnp.int32)
    chosen_mask = jnp.any(chosen[:, None] == block_ids[None, :], axis=0).astype(jnp.float32)
    outgoing = picked * chosen_mask[:, None]
    rebuilt = inverse_blocks(cosine, scatter_coefs(outgoing, coef_index).reshape(n_blocks, 64, 64))
    new_error = from_blocks(blocks - rebuilt, shard_rows, columns).astype(jnp.bfloat16)[None]
    earlier = (owner_map[None, :] == owner_map[:, None]) & (block_ids[None, :] < block_ids[:, None])
    slot_of = jnp.sum(earlier.astype(jnp.int32), axis=1)
    target = owner_map * capacity + slot_of
    own_slots = my_island * capacity + jnp.arange(capacity, dtype=jnp.int32)
    owned_mask = target[None, :] == own_slots[:, None]
    owned_ids = jnp.sum(jnp.where(owned_mask, block_ids[None, :], 0), axis=1)
    owned_live = jnp.any(owned_mask, axis=1)
    owned_pattern = jnp.sum(jnp.where(owned_mask[:, :, None], coef_index[None, :, :], 0), axis=1)
    listed = outgoing[chosen]
    piece_values = lax.all_gather(listed, "island", axis=0, tiled=True)
    piece_ids = lax.all_gather(chosen, "island", axis=0, tiled=True)
    matches = ((piece_ids[None, :] == owned_ids[:, None]) & owned_live[:, None]).astype(jnp.float32)
    totals = jnp.dot(matches, piece_values, precision=precise_mode)
    counts = jnp.sum(matches, axis=1)
    average = totals / jnp.maximum(counts, 1.0)[:, None]
    previous = momentum[0].reshape(capacity, coef_total)
    refreshed = BETA_FACTOR * previous + average
    update_coef = average + BETA_FACTOR * refreshed
    new_momentum = refreshed.reshape(1, capacity * coef_total)
    owner_dense = inverse_blocks(
        cosine, scatter_coefs(update_coef, owned_pattern).reshape(capacity, 64, 64)
    )
    owner_dense = owner_dense.reshape(capacity, 4096).astype(jnp.bfloat16)
    gathered_dense = lax.all_gather(owner_dense, "island", axis=0, tiled=True)
    selector = (target[:, None] == jnp.arange(islands * capacity, dtype=jnp.int32)[None, :]).astype(
        jnp.bfloat16
    )
    received = jnp.dot(selector, gathered_dense, preferred_element_type=jnp.float32)
    local_square = jnp.sum(received * received)
    total_square = lax.psum(local_square, "fsdp")
    scale_root = jnp.sqrt(total_square / (shard_rows * lax.axis_size("fsdp") * columns) + EPSILON)
    shifted = from_blocks(received.reshape(n_blocks, 64, 64), shard_rows, columns)
    new_params = (params.astype(jnp.float32) - OUTER_RATE * shifted / scale_root).astype(
        jnp.bfloat16
    )
    return (new_params, new_error, new_momentum)


def solution(mesh):
    in_specs = (
        P("island", "fsdp", None),
        P("island", "fsdp", None),
        P("fsdp", None),
        P("island", "fsdp"),
        P("island", "fsdp"),
        P("fsdp", None),
        P("fsdp"),
    )
    out_specs = (P("fsdp", None), P("island", "fsdp", None), P("island", "fsdp"))
    return jax.shard_map(
        on_device, mesh=mesh, in_specs=in_specs, out_specs=out_specs, check_vma=False
    )
```

profile of v0, /device:TPU:4, one launch (start us, length us, event | category | flops | bytes accessed | tf_op | source)
XLA Modules:
  0.0 641.8 jit_solution(827042617900372828)
XLA Ops:
  7.2 0.7 fusion.42
  7.9 0.7 fusion.19
  8.7 0.8 copy.69
  9.6 1.8 convert_add_fusion
  11.5 2.4 add.99
  13.8 2.9 copy.72
  16.8 1.9 copy-done
  18.7 8.3 %fusion.17 = f32[128,64,64]{2,1,0:T(8,128)} fusion(f32[128,64,64]{2,1,0:T(8,128)S(1)} %bitcast.58, f32[64]{0:T(128)S(1)} %get-tuple-element.10, f32[64]{0:T(128)S(1)} %get-tuple-element.9), kind=kOutput, calls=%fused_computation.39 | convolution fusion | flops 402665472 | bytes 4194816 | tf_op jit(solution)/shard_map/ij,bjk,lk->bil/dot_general | solution.py:40
  27.0 5.4 copy.75
  32.3 3.7 fusion.15
  36.1 52.5 %gather_fusion.1 = f32[8192]{0:T(1024)S(1)} fusion(f32[128,4096]{0,1:T(8,128)S(1)} %bitcast.57, s32[8192]{0:T(1024)S(1)} %reshape.187), kind=kCustom, calls=%fused_computation.1 | custom fusion | bytes 131072 | tf_op jit(solution)/shard_map/jit(take_along_axis)/gather | solution.py:68
  88.7 0.1 select_multiply_fusion
  88.8 1.2 gather_fusion
  90.2 0.2 convert_reduce_fusion
  90.4 0.2 select_reduce_fusion.1
  90.5 0.1 reduce_or.18
  90.7 0.1 select_reduce_fusion
  90.9 1.3 dynamic-slice
  92.8 0.1 bitcast_dynamic-update-slice_fusion
  93.0 323.1 %all-reduce = s32[6144]{0:T(1024)S(1)} all-reduce(s32[6144]{0:T(1024)S(1)} %bitcast_dynamic-update-slice_fusion), channel_id=2, replica_groups=mesh['island'=96,'fsdp'=8] {'island'}, use_global_device_ids=true, to_apply=%add | all-reduce | flops 6144 | bytes 49152
  416.0 0.2 fusion.7
  416.3 3.0 multiply_add_fusion
  419.4 6.7 %scatter_fusion = f32[2,4096]{1,0:T(2,128)S(1)} fusion(f32[2,4096]{1,0:T(2,128)S(1)} %broadcast_in_dim.52, s32[128]{0:T(128)S(1)} %reshape.193, f32[128]{0:T(128)S(1)} %reshape.195), kind=kCustom, calls=%fused_computation.2 | custom fusion | bytes 2560 | tf_op jit(solution)/shard_map/scatter | solution.py:52
  426.1 0.1 reshape.171
  426.2 0.4 fusion.13
  426.6 0.4 convolution_convert_fusion
  427.0 0.7 reshape.210
  427.8 3.8 copy.85
  431.7 0.1 multiply_reduce_fusion.1
  431.8 0.1 and_reduce_fusion
  432.0 31.9 %scatter_custom_fusion.1 = f32[524288]{0:T(1024)} fusion(s32[8192]{0:T(1024)S(1)} %reshape.199, f32[8192]{0:T(1024)S(1)} %reshape.201, f32[]{:T(128)} %constant.22.clone.1), kind=kCustom, calls=%fused_computation.11 | custom fusion | bytes 2097156
  463.8 4.3 reshape.172
  468.2 9.9 %fusion.10 = f32[128,64,64]{2,1,0:T(8,128)} fusion(f32[128,64,64]{2,1,0:T(8,128)} %reshape.172, f32[64]{0:T(128)S(1)} %get-tuple-element.10, f32[64]{0:T(128)S(1)} %get-tuple-element.9), kind=kOutput, calls=%fused_computation.32 | convolution fusion | flops 402665472 | bytes 4194816 | tf_op jit(solution)/shard_map/ji,bjk,kl->bil/dot_general | solution.py:44
  478.1 5.3 copy.84
  483.4 3.9 subtract_convert_fusion
  487.3 3.0 copy.86
  490.3 3.2 copy.87
  493.4 4.0 convert_element_type.67
  497.5 0.6 reshape.173
  498.0 96.6 %all-gather.8.cloned.1.call-done = bf16[96,2,4096]{2,1,0:T(2,128)(2,1)} async-done(((bf16[1,2,4096]{2,1,0:T(2,128)(2,1)}), bf16[96,2,4096]{2,1,0:T(2,128)(2,1)}) %all-gather.8.cloned.1.call-update) | async-done | bytes 1572880 | tf_op jit(solution)/shard_map/all_gather | solution.py:98
  594.7 2.5 reshape.211
  597.2 2.4 multiply_reduce_fusion
  599.6 17.6 %psum.7 = f32[]{:T(128)} all-reduce(f32[]{:T(128)} %get-tuple-element.7), channel_id=1, replica_groups=mesh['island'=96,'fsdp'=8] {'fsdp'}, use_global_device_ids=true, to_apply=%region_8.9 | all-reduce | flops 1 | bytes 8 | tf_op jit(solution)/shard_map/psum | solution.py:104
  617.9 1.8 multiply_divide_fusion
  619.7 3.0 div.49
  622.7 7.4 %copy.81 = f32[16,64,8,64]{3,2,1,0:T(8,128)} copy(f32[16,64,8,64]{3,1,2,0:T(8,128)} %bitcast.60) | data formatting | bytes 4194304 | tf_op jit(solution)/shard_map/div | solution.py:107
  630.1 3.5 div.51
  633.7 1.3 subtract_convert_fusion.1
  (41 shorter events, 0.9 us)
Async XLA Ops:
  7.2 409.1 %all-gather.6.cloned.1.call-start = ((), (), s32[]{:S(2)}) async-start(), calls=%async_computation | async-start | bytes 3178496 | tf_op jit(solution)/shard_map/all_gather | solution.py:84
  16.8 1.9 copy-start
  36.0 54.0 %copy-start.5 = (f32[1,128]{1,0:T(1,128)S(1)}, f32[1,128]{1,0:T(1,128)}, u32[]{:S(2)}) copy-start(f32[1,128]{1,0:T(1,128)} %param.10) | copy-start | bytes 1540
  36.0 54.1 %copy-start.6 = (s32[128]{0:T(128)S(1)}, s32[128]{0:T(128)}, u32[]{:S(2)}) copy-start(s32[128]{0:T(128)} %param.13) | copy-start | bytes 1540
  36.0 54.6 %copy-start.2 = (s32[128,64]{0,1:T(8,128)S(1)}, s32[128,64]{0,1:T(8,128)}, u32[]{:S(2)}) copy-start(s32[128,64]{0,1:T(8,128)} %param.12) | copy-start | bytes 98308
  36.1 56.8 %copy-start.7 = (s32[1,64]{1,0:T(1,128)S(1)}, s32[1,64]{1,0:T(1,128)}, u32[]{:S(2)}) copy-start(s32[1,64]{1,0:T(1,128)} %param.11) | copy-start | bytes 772
  90.0 504.7 %all-gather.8.cloned.1.call-start = ((), (), s32[]{:S(2)}) async-start(), calls=%async_computation.1 | async-start | bytes 1589248 | tf_op jit(solution)/shard_map/all_gather | solution.py:98
  427.7 3.9 copy-start.4
  427.7 4.0 copy-start.3
  630.1 3.5 copy-start.1
Sparse Core Ops, SparseCore 0:
  90.1 122.9 all-gather.5
  427.8 166.7 all-gather.7
where the time goes:
time: 643 us; the launch traced here: 642 us
  blocking collectives  341 us (53%)
  local copies, waits for them, and re-layouts  149 us (23%)
  waiting for transfers between devices  96.7 us (15%)
  matrix products  32 us (5%)
  between operations  15.7 us (2%)
  other arithmetic  7.56 us (1%)
    unnamed x1, blocking collectives  323 us
    all_gather x1, waiting for transfers between devices, on_device(): gathered_dense = lax.all_gather(owner_dense, 'island', axis=0, tiled=True)  96.6 us
    gather x4, local copies, waits for them, and re-layouts, on_device(): picked = jnp.take_along_axis(spectra, coef_index, axis=1)  52.7 us
    unnamed x24, local copies, waits for them, and re-layouts  39.4 us
    psum x1, blocking collectives, on_device(): total_square = lax.psum(local_square, 'fsdp')  17.6 us
    dot_general x4, matrix products, inverse_blocks(): jnp.einsum('ji,bjk,kl->bil', cosine, blocks, cosine, precision=precise_mode)  14.5 us
    div x3, local copies, waits for them, and re-layouts, on_device(): OUTER_RATE * shifted / scale_root  13.9 us
  transfers between devices with their start and end apart: 2, of which 1 were waited for; matrix products, arithmetic and copies ran while one was open for 11% of the time, Pallas kernels for 0%

commit v1 on v0

v1 whole, which is shorter than its diff:
```python
import functools

import jax
import jax.numpy as jnp
from jax import lax
from jax.sharding import PartitionSpec as P

BETA_FACTOR = 0.9
OUTER_RATE = 0.5
EPSILON = 1e-06
precise_mode = lax.Precision.HIGHEST


def cosine_table():
    freqs = jnp.arange(64, dtype=jnp.float32)[:, None]
    points = jnp.arange(64, dtype=jnp.float32)[None, :]
    scaling = jnp.where(freqs == 0.0, jnp.sqrt(1.0 / 64.0), jnp.sqrt(2.0 / 64.0))
    return scaling * jnp.cos(jnp.pi * (2.0 * points + 1.0) * freqs / 128.0)


def to_blocks(field):
    row_blocks = field.shape[0] // 64
    col_blocks = field.shape[1] // 64
    return (
        field.reshape(row_blocks, 64, col_blocks, 64)
        .transpose(0, 2, 1, 3)
        .reshape(row_blocks * col_blocks, 64, 64)
    )


def from_blocks(blocks, row_total, col_total):
    row_blocks = row_total // 64
    col_blocks = col_total // 64
    return (
        blocks.reshape(row_blocks, col_blocks, 64, 64)
        .transpose(0, 2, 1, 3)
        .reshape(row_total, col_total)
    )


def one_hot_rows(table, index):
    hot = (index[..., None] == jnp.arange(table.shape[0], dtype=jnp.int32)).astype(jnp.float32)
    return jnp.einsum("...t,tc->...c", hot, table, precision=precise_mode)


def decode(row_cos, col_cos, values):
    return jnp.einsum("bkj,bkl->bjl", row_cos * values[:, :, None], col_cos, precision=precise_mode)


def butterfly_sum(value, axis, radices):
    size = lax.axis_size(axis)
    here = lax.axis_index(axis)
    stride = 1
    for radix in radices:
        digit = (here // stride) % radix
        pieces = {0: value}
        for shift in range(1, radix):
            perm = []
            for src in range(size):
                d = (src // stride) % radix
                perm.append((src, src + ((d + shift) % radix - d) * stride))
            pieces[shift] = lax.ppermute(value, axis, perm)
        if radix == 2:
            value = pieces[0] + pieces[1]
        else:
            ordered = []
            for e in range(radix):
                pick = pieces[0]
                for shift in range(1, radix):
                    pick = jnp.where((digit - shift) % radix == e, pieces[shift], pick)
                ordered.append(pick)
            value = ordered[0]
            for e in range(1, radix):
                value = value + ordered[e]
        stride *= radix
    return value


def radices_of(sub_sizes):
    out = []
    for part in reversed(sub_sizes):
        left = part
        for prime in (2, 3, 5, 7):
            while left % prime == 0:
                out.append(prime)
                left //= prime
        if left > 1:
            out.append(left)
    return out


def on_device(island_radices, fsdp_radices, pseudo_grad, error_buf, params, momentum, sel_blocks, coef_index, owner_map):
    cosine = cosine_table()
    my_island = lax.axis_index("island")
    shard_rows = params.shape[0]
    columns = params.shape[1]
    n_blocks = coef_index.shape[0]
    coef_total = coef_index.shape[1]
    capacity = momentum.shape[1] // coef_total

    summed = pseudo_grad[0].astype(jnp.float32) + error_buf[0].astype(jnp.float32)
    blocks = to_blocks(summed)
    row_cos = one_hot_rows(cosine, coef_index // 64)
    col_cos = one_hot_rows(cosine, coef_index % 64)
    half = jnp.einsum("bkj,bjl->bkl", row_cos, blocks, precision=precise_mode)
    picked = jnp.sum(half * col_cos, axis=2)

    chosen = sel_blocks[0]
    block_ids = jnp.arange(n_blocks, dtype=jnp.int32)
    chosen_mask = jnp.any(chosen[:, None] == block_ids[None, :], axis=0).astype(jnp.float32)
    outgoing = picked * chosen_mask[:, None]

    earlier = (owner_map[None, :] == owner_map[:, None]) & (block_ids[None, :] < block_ids[:, None])
    slot_of = jnp.sum(earlier.astype(jnp.int32), axis=1)
    target = owner_map * capacity + slot_of
    own_slots = my_island * capacity + jnp.arange(capacity, dtype=jnp.int32)
    owned_mask = (target[None, :] == own_slots[:, None]).astype(jnp.float32)
    mine = momentum[0].reshape(capacity, coef_total)
    held = jnp.einsum("sb,sk->bk", owned_mask, mine, precision=precise_mode)

    mask_rows = -(-n_blocks // coef_total)
    mask_part = jnp.pad(chosen_mask, (0, mask_rows * coef_total - n_blocks)).reshape(mask_rows, coef_total)
    payload = jnp.concatenate([outgoing, held, mask_part], axis=0)
    reduced = butterfly_sum(payload, "island", island_radices)
    totals = reduced[:n_blocks]
    previous = reduced[n_blocks : 2 * n_blocks]
    counts = reduced[2 * n_blocks :].reshape(-1)[:n_blocks]

    rebuilt = decode(row_cos, col_cos, outgoing)
    new_error = from_blocks(blocks - rebuilt, shard_rows, columns).astype(jnp.bfloat16)[None]

    average = totals / jnp.maximum(counts, 1.0)[:, None]
    refreshed = BETA_FACTOR * previous + average
    update_coef = average + BETA_FACTOR * refreshed

    owned_live = jnp.sum(owned_mask, axis=1) > 0.0
    owned_fresh = jnp.dot(owned_mask, refreshed, precision=precise_mode)
    kept = BETA_FACTOR * mine
    new_momentum = jnp.where(owned_live[:, None], owned_fresh, kept).reshape(1, capacity * coef_total)

    update = decode(row_cos, col_cos, update_coef).astype(jnp.bfloat16).astype(jnp.float32)
    local_square = jnp.sum(update * update)
    total_square = butterfly_sum(local_square, "fsdp", fsdp_radices)
    scale_root = jnp.sqrt(total_square / (shard_rows * lax.axis_size("fsdp") * columns) + EPSILON)
    shifted = from_blocks(update, shard_rows, columns)
    new_params = (params.astype(jnp.float32) - OUTER_RATE * shifted / scale_root).astype(
        jnp.bfloat16
    )
    return (new_params, new_error, new_momentum)


def solution(mesh):
    in_specs = (
        P("island", "fsdp", None),
        P("island", "fsdp", None),
        P("fsdp", None),
        P("island", "fsdp"),
        P("island", "fsdp"),
        P("fsdp", None),
        P("fsdp"),
    )
    out_specs = (P("fsdp", None), P("island", "fsdp", None), P("island", "fsdp"))
    island_radices = radices_of((4, 12, 2))
    if mesh.shape["island"] != 96:
        island_radices = radices_of((mesh.shape["island"],))
    fsdp_radices = radices_of((mesh.shape["fsdp"],))
    body = functools.partial(on_device, island_radices, fsdp_radices)
    return jax.shard_map(
        body, mesh=mesh, in_specs=in_specs, out_specs=out_specs, check_vma=False
    )
```

time: 643 us -> 193 us (0.30)
  the two profiles are of different devices: /device:TPU:4 before, /device:TPU:192 now
where the time goes in v1:
time: 193 us; the launch traced here: 190 us
  local copies, waits for them, and re-layouts  47.4 us (25%)
  starting transfers between devices  47.4 us (25%)
  waiting for transfers between devices  40.2 us (21%)
  matrix products  38.4 us (20%)
  other arithmetic  12.5 us (6%)
  between operations  3.92 us (2%)
    ppermute x10, starting transfers between devices, butterfly_sum(): pieces[shift] = lax.ppermute(value, axis, perm)  47.4 us
    ppermute x10, waiting for transfers between devices, butterfly_sum(): pieces[shift] = lax.ppermute(value, axis, perm)  40.2 us
    dot_general x2, matrix products, decode(): jnp.einsum('bkj,bkl->bjl', row_cos * values[:, :, None], col_cos, precisi...  22.4 us
    dot_general x1, matrix products, on_device(): half = jnp.einsum('bkj,bjl->bkl', row_cos, blocks, precision=precise_mode)  11.6 us
    dot_general x2, local copies, waits for them, and re-layouts, one_hot_rows(): return jnp.einsum('...t,tc->...c', hot, table, precision=precise_mode)  10.4 us
    mul x2, local copies, waits for them, and re-layouts, decode(): row_cos * values[:, :, None]  10.3 us
    add x2, local copies, waits for them, and re-layouts, on_device(): pseudo_grad[0].astype(jnp.float32) + error_buf[0].astype(jnp.float32)  9.27 us
    div x2, local copies, waits for them, and re-layouts, on_device(): OUTER_RATE * shifted / scale_root  8.72 us
  transfers between devices with their start and end apart: 10, of which 10 were waited for; matrix products, arithmetic and copies ran while one was open for 0% of the time, Pallas kernels for 0%

profile of v1, /device:TPU:192, one launch (start us, length us, event | category | flops | bytes accessed | tf_op | source)
XLA Modules:
  0.0 189.8 jit_solution(13397795341020861171)
XLA Ops:
  0.7 0.5 broadcast.110
  1.2 1.3 reduce.3
  2.6 0.7 fusion.12
  3.3 0.9 convert_reduce_fusion
  4.2 0.7 multiply_add_fusion.1
  5.0 0.8 add_select_fusion
  5.8 2.6 %fusion.3 = f32[128,64,64]{0,2,1:T(8,128)} fusion(s32[128,64]{0,1:T(8,128)S(1)} %get-tuple-element.5, f32[64]{0:T(128)S(1)} %get-tuple-element.10, f32[64]{0:T(128)S(1)} %get-tuple-element.9), kind=kOutput, calls=%fused_computation.11 | convolution fusion | flops 403189760 | bytes 2130432 | tf_op jit(solution)/shard_map/...t,tc->...c/dot_general | solution.py:43
  8.4 1.2 fusion.2
  9.6 5.9 %copy.51 = f32[128,64,64]{1,2,0:T(8,128)} copy(f32[128,64,64]{0,2,1:T(8,128)} %fusion.3) | data formatting | bytes 4194304 | tf_op jit(solution)/shard_map/...t,tc->...c/dot_general | solution.py:43
  15.5 2.9 %convert_add_fusion = f32[1,1024,512]{2,1,0:T(8,128)} fusion(bf16[1,1024,512]{2,1,0:T(8,128)(2,1)S(1)} %copy-done.1, bf16[1,1024,512]{2,1,0:T(8,128)(2,1)} %param.7), kind=kLoop, calls=%fused_computation.8 | loop fusion | flops 1572864 | bytes 4194304 | tf_op jit(solution)/shard_map/add | solution.py:101
  18.4 4.4 %add.101 = f32[16,64,8,64]{3,2,1,0:T(8,128)} reshape(f32[1,1024,512]{2,1,0:T(8,128)} %convert_add_fusion) | data formatting | bytes 4194304 | tf_op jit(solution)/shard_map/add | solution.py:101
  22.7 4.9 %copy.48 = f32[16,64,8,64]{3,1,2,0:T(8,128)} copy(f32[16,64,8,64]{3,2,1,0:T(8,128)} %add.101) | data formatting | bytes 4194304 | tf_op jit(solution)/shard_map/add | solution.py:101
  27.6 4.5 %copy.49 = f32[128,64,64]{2,1,0:T(8,128)} copy(f32[128,64,64]{0,2,1:T(8,128)S(1)} %fusion.2) | data formatting | bytes 4194304 | tf_op jit(solution)/shard_map/...t,tc->...c/dot_general | solution.py:43
  32.1 11.6 %multiply_reduce_fusion = f32[128,64]{1,0:T(8,128)S(1)} fusion(f32[128,64,64]{1,2,0:T(8,128)} %copy.51, f32[128,64,64]{2,1,0:T(8,128)} %copy.49, f32[128,64,64]{2,1,0:T(8,128)} %bitcast.26), kind=kOutput, calls=%fused_computation.5 | convolution fusion | flops 403693568 | bytes 6324224 | tf_op jit(solution)/shard_map/bkj,bjl->bkl/dot_general | solution.py:105
  43.9 0.3 fusion.21
  44.2 1.9 %collective-permute-start = (f32[258,64]{1,0:T(8,128)S(1)}, f32[258,64]{1,0:T(8,128)S(1)}, u32[]{:S(2)}, u32[]{:S(2)}) collective-permute-start(f32[258,64]{1,0:T(8,128)S(1)} %pad_maximum_fusion), channel_id=1, source_target_pairs={{0,8},{8,0},{16,24},{24,16},{32,40},{40,32},{48,56},{56,48},{64,72... | collective-permute-start | bytes 198152 | tf_op jit(solution)/shard_map/ppermute | solution.py:62
  46.1 1.3 collective-permute-done
  47.5 1.9 %collective-permute-start.1 = (f32[258,64]{1,0:T(8,128)S(1)}, f32[258,64]{1,0:T(8,128)S(1)}, u32[]{:S(2)}, u32[]{:S(2)}) collective-permute-start(f32[258,64]{1,0:T(8,128)S(1)} %fusion.31), channel_id=1, source_target_pairs={{0,16},{8,24},{16,0},{24,8},{32,48},{40,56},{48,32},{56,40},{64,80... | collective-permute-start | bytes 198152 | tf_op jit(solution)/shard_map/ppermute | solution.py:62
  49.4 5.6 %collective-permute-done.1 = f32[258,64]{1,0:T(8,128)S(1)} collective-permute-done((f32[258,64]{1,0:T(8,128)S(1)}, f32[258,64]{1,0:T(8,128)S(1)}, u32[]{:S(2)}, u32[]{:S(2)}) %collective-permute-start.1) | collective-permute-done | bytes 66080 | tf_op jit(solution)/shard_map/ppermute | solution.py:62
  55.0 7.6 %collective-permute-start.2 = (f32[258,64]{1,0:T(8,128)S(1)}, f32[258,64]{1,0:T(8,128)S(1)}, u32[]{:S(2)}, u32[]{:S(2)}) collective-permute-start(f32[258,64]{1,0:T(8,128)S(1)} %add.107), channel_id=1, source_target_pairs={{0,32},{8,40},{16,48},{24,56},{32,0},{40,8},{48,16},{56,24},{64,96... | collective-permute-start | bytes 198152 | tf_op jit(solution)/shard_map/ppermute | solution.py:62
  62.6 6.2 %collective-permute-done.2 = f32[258,64]{1,0:T(8,128)S(1)} collective-permute-done((f32[258,64]{1,0:T(8,128)S(1)}, f32[258,64]{1,0:T(8,128)S(1)}, u32[]{:S(2)}, u32[]{:S(2)}) %collective-permute-start.2) | collective-permute-done | bytes 66080 | tf_op jit(solution)/shard_map/ppermute | solution.py:62
  68.8 7.9 %collective-permute-start.4 = (f32[258,64]{1,0:T(8,128)S(1)}, f32[258,64]{1,0:T(8,128)S(1)}, u32[]{:S(2)}, u32[]{:S(2)}) collective-permute-start(f32[258,64]{1,0:T(8,128)S(1)} %add.108), channel_id=1, source_target_pairs={{0,64},{8,72},{16,80},{24,88},{32,96},{40,104},{48,112},{56,120},{... | collective-permute-start | bytes 198152 | tf_op jit(solution)/shard_map/ppermute | solution.py:62
  76.7 3.1 %collective-permute-start.3 = (f32[258,64]{1,0:T(8,128)S(1)}, f32[258,64]{1,0:T(8,128)S(1)}, u32[]{:S(2)}, u32[]{:S(2)}) collective-permute-start(f32[258,64]{1,0:T(8,128)S(1)} %add.108), channel_id=1, source_target_pairs={{0,128},{8,136},{16,144},{24,152},{32,160},{40,168},{48,176},{56,1... | collective-permute-start | bytes 198152 | tf_op jit(solution)/shard_map/ppermute | solution.py:62
  79.9 7.9 %collective-permute-done.4 = f32[258,64]{1,0:T(8,128)S(1)} collective-permute-done((f32[258,64]{1,0:T(8,128)S(1)}, f32[258,64]{1,0:T(8,128)S(1)}, u32[]{:S(2)}, u32[]{:S(2)}) %collective-permute-start.4) | collective-permute-done | bytes 66080 | tf_op jit(solution)/shard_map/ppermute | solution.py:62
  87.8 7.4 %collective-permute-done.3 = f32[258,64]{1,0:T(8,128)S(1)} collective-permute-done((f32[258,64]{1,0:T(8,128)S(1)}, f32[258,64]{1,0:T(8,128)S(1)}, u32[]{:S(2)}, u32[]{:S(2)}) %collective-permute-start.3) | collective-permute-done | bytes 66080 | tf_op jit(solution)/shard_map/ppermute | solution.py:62
  95.3 3.1 %collective-permute-start.5 = (f32[258,64]{1,0:T(8,128)S(1)}, f32[258,64]{1,0:T(8,128)S(1)}, u32[]{:S(2)}, u32[]{:S(2)}) collective-permute-start(f32[258,64]{1,0:T(8,128)S(1)} %select_add_fusion), channel_id=1, source_target_pairs={{0,192},{8,200},{16,208},{24,216},{32,224},{40,232},{48,240},{56,2... | collective-permute-start | bytes 198152 | tf_op jit(solution)/shard_map/ppermute | solution.py:62
  98.6 4.1 %collective-permute-done.5 = f32[258,64]{1,0:T(8,128)S(1)} collective-permute-done((f32[258,64]{1,0:T(8,128)S(1)}, f32[258,64]{1,0:T(8,128)S(1)}, u32[]{:S(2)}, u32[]{:S(2)}) %collective-permute-start.5) | collective-permute-done | bytes 66080 | tf_op jit(solution)/shard_map/ppermute | solution.py:62
  102.7 4.6 %collective-permute-start.6 = (f32[258,64]{1,0:T(8,128)S(1)}, f32[258,64]{1,0:T(8,128)S(1)}, u32[]{:S(2)}, u32[]{:S(2)}) collective-permute-start(f32[258,64]{1,0:T(8,128)S(1)} %add.112), channel_id=1, source_target_pairs={{0,384},{8,392},{16,400},{24,408},{32,416},{40,424},{48,432},{56,4... | collective-permute-start | bytes 198152 | tf_op jit(solution)/shard_map/ppermute | solution.py:62
  107.4 3.7 %collective-permute-done.6 = f32[258,64]{1,0:T(8,128)S(1)} collective-permute-done((f32[258,64]{1,0:T(8,128)S(1)}, f32[258,64]{1,0:T(8,128)S(1)}, u32[]{:S(2)}, u32[]{:S(2)}) %collective-permute-start.6) | collective-permute-done | bytes 66080 | tf_op jit(solution)/shard_map/ppermute | solution.py:62
  111.3 0.2 convolution_select_fusion
  111.6 0.6 reshape.105
  112.2 2.8 %broadcast_multiply_fusion = (f32[128,64,64]{0,2,1:T(8,128)}, f32[128,64,64]{0,2,1:T(8,128)}) fusion(f32[128,64,64]{0,2,1:T(8,128)S(1)} %fusion.2, f32[128,64]{0,1:T(8,128)S(1)} %copy.57, f32[128,64]{0,1:T(8,128)S(1)} %copy.53), kind=kLoop, calls=%fused_computation.14 | loop fusion | flops 1048576 | bytes 6356992 | tf_op jit(solution)/shard_map/mul | solution.py:47
  115.0 5.6 %copy.58 = f32[128,64,64]{1,2,0:T(8,128)} copy(f32[128,64,64]{0,2,1:T(8,128)} %get-tuple-element.3) | data formatting | bytes 4194304 | tf_op jit(solution)/shard_map/mul | solution.py:47
  120.6 11.5 %subtract_convert_fusion = bf16[128,64,64]{2,1,0:T(8,128)(2,1)S(1)} fusion(f32[128,64,64]{2,1,0:T(8,128)} %bitcast.27, f32[128,64,64]{1,2,0:T(8,128)} %copy.58, f32[128,64,64]{1,2,0:T(8,128)} %copy.51), kind=kOutput, calls=%fused_computation.4 | convolution fusion | flops 403701760 | bytes 7340032 | tf_op jit(solution)/shard_map/bkj,bkl->bjl/dot_general | solution.py:47
  132.1 3.2 %copy.60 = bf16[16,64,8,64]{3,2,1,0:T(8,128)(2,1)} copy(bf16[16,64,8,64]{3,1,2,0:T(8,128)(2,1)S(1)} %bitcast.29) | data formatting | bytes 2097152 | tf_op jit(solution)/shard_map/convert_element_type | solution.py:130
  135.3 4.0 %convert_element_type.75 = bf16[1,1024,512]{2,1,0:T(8,128)(2,1)} reshape(bf16[16,64,8,64]{3,2,1,0:T(8,128)(2,1)} %copy.60) | data formatting | bytes 2097152 | tf_op jit(solution)/shard_map/convert_element_type | solution.py:130
  139.3 4.7 %copy.54 = f32[128,64,64]{1,2,0:T(8,128)} copy(f32[128,64,64]{0,2,1:T(8,128)S(1)} %copy-done) | data formatting | bytes 4194304 | tf_op jit(solution)/shard_map/mul | solution.py:47
  144.0 10.9 %fusion.1 = (f32[]{:T(128)}, bf16[128,64,64]{2,1,0:T(8,128)(2,1)S(1)}) fusion(f32[128,64,64]{1,2,0:T(8,128)} %copy.54, f32[128,64,64]{1,2,0:T(8,128)} %copy.51), kind=kOutput, calls=%fused_computation.3 | convolution fusion | flops 404750336 | bytes 5242884 | tf_op jit(solution)/shard_map/bkj,bkl->bjl/dot_general | solution.py:47
  154.9 3.2 %collective-permute-start.7 = (f32[]{:T(128)}, f32[]{:T(128)}, u32[]{:S(2)}, u32[]{:S(2)}) collective-permute-start(f32[]{:T(128)} %get-tuple-element.7), channel_id=1, source_target_pairs={{0,1},{1,0},{2,3},{3,2},{4,5},{5,4},{6,7},{7,6},{8,9},{9,8},{10,11... | collective-permute-start | bytes 20 | tf_op jit(solution)/shard_map/ppermute | solution.py:62
  158.1 2.4 %collective-permute-done.7 = f32[]{:T(128)} collective-permute-done((f32[]{:T(128)}, f32[]{:T(128)}, u32[]{:S(2)}, u32[]{:S(2)}) %collective-permute-start.7) | collective-permute-done | bytes 36 | tf_op jit(solution)/shard_map/ppermute | solution.py:62
  161.8 5.5 %collective-permute-start.8 = (f32[]{:T(128)}, f32[]{:T(128)}, u32[]{:S(2)}, u32[]{:S(2)}) collective-permute-start(f32[]{:T(128)} %add.116), channel_id=1, source_target_pairs={{0,2},{1,3},{2,0},{3,1},{4,6},{5,7},{6,4},{7,5},{8,10},{9,11},{10,... | collective-permute-start | bytes 20 | tf_op jit(solution)/shard_map/ppermute | solution.py:62
  167.2 0.9 collective-permute-done.8
  168.8 8.7 %collective-permute-start.9 = (f32[]{:T(128)}, f32[]{:T(128)}, u32[]{:S(2)}, u32[]{:S(2)}) collective-permute-start(f32[]{:T(128)} %add.117), channel_id=1, source_target_pairs={{0,4},{1,5},{2,6},{3,7},{4,0},{5,1},{6,2},{7,3},{8,12},{9,13},{10,... | collective-permute-start | bytes 20 | tf_op jit(solution)/shard_map/ppermute | solution.py:62
  177.5 0.6 collective-permute-done.9
  178.9 0.6 fusion
  179.5 5.2 %copy.56 = f32[16,64,8,64]{3,2,1,0:T(8,128)} copy(f32[16,64,8,64]{3,1,2,0:T(8,128)S(1)} %bitcast.28) | data formatting | bytes 4194304 | tf_op jit(solution)/shard_map/div | solution.py:146
  184.7 3.5 %div.70 = f32[1024,512]{1,0:T(8,128)S(1)} reshape(f32[16,64,8,64]{3,2,1,0:T(8,128)} %copy.56) | data formatting | bytes 4194304 | tf_op jit(solution)/shard_map/div | solution.py:146
  188.2 1.3 subtract_convert_fusion.1
  (26 shorter events, 1.0 us)
Async XLA Ops:
  8.4 7.2 %copy-start.1 = (bf16[1,1024,512]{2,1,0:T(8,128)(2,1)S(1)}, bf16[1,1024,512]{2,1,0:T(8,128)(2,1)}, u32[]{:S(2)}) copy-start(bf16[1,1024,512]{2,1,0:T(8,128)(2,1)} %param.8) | copy-start | bytes 3145732
  44.2 3.2 %collective-permute-start = (f32[258,64]{1,0:T(8,128)S(1)}, f32[258,64]{1,0:T(8,128)S(1)}, u32[]{:S(2)}, u32[]{:S(2)}) collective-permute-start(f32[258,64]{1,0:T(8,128)S(1)} %pad_maximum_fusion), channel_id=1, source_target_pairs={{0,8},{8,0},{16,24},{24,16},{32,40},{40,32},{48,56},{56,48},{64,72... | collective-permute-start | bytes 198152 | tf_op jit(solution)/shard_map/ppermute | solution.py:62
  47.5 7.5 %collective-permute-start.1 = (f32[258,64]{1,0:T(8,128)S(1)}, f32[258,64]{1,0:T(8,128)S(1)}, u32[]{:S(2)}, u32[]{:S(2)}) collective-permute-start(f32[258,64]{1,0:T(8,128)S(1)} %fusion.31), channel_id=1, source_target_pairs={{0,16},{8,24},{16,0},{24,8},{32,48},{40,56},{48,32},{56,40},{64,80... | collective-permute-start | bytes 198152 | tf_op jit(solution)/shard_map/ppermute | solution.py:62
  55.0 13.8 %collective-permute-start.2 = (f32[258,64]{1,0:T(8,128)S(1)}, f32[258,64]{1,0:T(8,128)S(1)}, u32[]{:S(2)}, u32[]{:S(2)}) collective-permute-start(f32[258,64]{1,0:T(8,128)S(1)} %add.107), channel_id=1, source_target_pairs={{0,32},{8,40},{16,48},{24,56},{32,0},{40,8},{48,16},{56,24},{64,96... | collective-permute-start | bytes 198152 | tf_op jit(solution)/shard_map/ppermute | solution.py:62
  68.8 19.0 %collective-permute-start.4 = (f32[258,64]{1,0:T(8,128)S(1)}, f32[258,64]{1,0:T(8,128)S(1)}, u32[]{:S(2)}, u32[]{:S(2)}) collective-permute-start(f32[258,64]{1,0:T(8,128)S(1)} %add.108), channel_id=1, source_target_pairs={{0,64},{8,72},{16,80},{24,88},{32,96},{40,104},{48,112},{56,120},{... | collective-permute-start | bytes 198152 | tf_op jit(solution)/shard_map/ppermute | solution.py:62
  76.7 18.6 %collective-permute-start.3 = (f32[258,64]{1,0:T(8,128)S(1)}, f32[258,64]{1,0:T(8,128)S(1)}, u32[]{:S(2)}, u32[]{:S(2)}) collective-permute-start(f32[258,64]{1,0:T(8,128)S(1)} %add.108), channel_id=1, source_target_pairs={{0,128},{8,136},{16,144},{24,152},{32,160},{40,168},{48,176},{56,1... | collective-permute-start | bytes 198152 | tf_op jit(solution)/shard_map/ppermute | solution.py:62
  95.3 7.4 %collective-permute-start.5 = (f32[258,64]{1,0:T(8,128)S(1)}, f32[258,64]{1,0:T(8,128)S(1)}, u32[]{:S(2)}, u32[]{:S(2)}) collective-permute-start(f32[258,64]{1,0:T(8,128)S(1)} %select_add_fusion), channel_id=1, source_target_pairs={{0,192},{8,200},{16,208},{24,216},{32,224},{40,232},{48,240},{56,2... | collective-permute-start | bytes 198152 | tf_op jit(solution)/shard_map/ppermute | solution.py:62
  102.7 8.4 %collective-permute-start.6 = (f32[258,64]{1,0:T(8,128)S(1)}, f32[258,64]{1,0:T(8,128)S(1)}, u32[]{:S(2)}, u32[]{:S(2)}) collective-permute-start(f32[258,64]{1,0:T(8,128)S(1)} %add.112), channel_id=1, source_target_pairs={{0,384},{8,392},{16,400},{24,408},{32,416},{40,424},{48,432},{56,4... | collective-permute-start | bytes 198152 | tf_op jit(solution)/shard_map/ppermute | solution.py:62
  132.1 7.2 %copy-start = (f32[128,64,64]{0,2,1:T(8,128)S(1)}, f32[128,64,64]{0,2,1:T(8,128)}, u32[]{:S(2)}) copy-start(f32[128,64,64]{0,2,1:T(8,128)} %get-tuple-element.4) | copy-start | bytes 6291460
  154.9 5.5 %collective-permute-start.7 = (f32[]{:T(128)}, f32[]{:T(128)}, u32[]{:S(2)}, u32[]{:S(2)}) collective-permute-start(f32[]{:T(128)} %get-tuple-element.7), channel_id=1, source_target_pairs={{0,1},{1,0},{2,3},{3,2},{4,5},{5,4},{6,7},{7,6},{8,9},{9,8},{10,11... | collective-permute-start | bytes 20 | tf_op jit(solution)/shard_map/ppermute | solution.py:62
  161.8 6.3 %collective-permute-start.8 = (f32[]{:T(128)}, f32[]{:T(128)}, u32[]{:S(2)}, u32[]{:S(2)}) collective-permute-start(f32[]{:T(128)} %add.116), channel_id=1, source_target_pairs={{0,2},{1,3},{2,0},{3,1},{4,6},{5,7},{6,4},{7,5},{8,10},{9,11},{10,... | collective-permute-start | bytes 20 | tf_op jit(solution)/shard_map/ppermute | solution.py:62
  168.8 9.3 %collective-permute-start.9 = (f32[]{:T(128)}, f32[]{:T(128)}, u32[]{:S(2)}, u32[]{:S(2)}) collective-permute-start(f32[]{:T(128)} %add.117), channel_id=1, source_target_pairs={{0,4},{1,5},{2,6},{3,7},{4,0},{5,1},{6,2},{7,3},{8,12},{9,13},{10,... | collective-permute-start | bytes 20 | tf_op jit(solution)/shard_map/ppermute | solution.py:62
  184.7 3.5 %copy-start.2 = (bf16[1024,512]{1,0:T(8,128)(2,1)S(1)}, bf16[1024,512]{1,0:T(8,128)(2,1)}, u32[]{:S(2)}) copy-start(bf16[1024,512]{1,0:T(8,128)(2,1)} %param.9) | copy-start | bytes 3145732

commit v2 on v1

--- a/solution.py
+++ b/solution.py
@@ -9,6 +9,8 @@
 OUTER_RATE = 0.5
 EPSILON = 1e-06
 precise_mode = lax.Precision.HIGHEST
+ERR_CHUNKS = 4
+UPD_CHUNKS = 2
 
 
 def cosine_table():
@@ -89,7 +91,11 @@
     return out
 
 
-def on_device(island_radices, fsdp_radices, pseudo_grad, error_buf, params, momentum, sel_blocks, coef_index, owner_map):
+def on_device(island_radices, fsdp_radices, *args):
+    return step_body(island_radices, fsdp_radices, *args)
+
+
+def step_body(island_radices, fsdp_radices, pseudo_grad, error_buf, params, momentum, sel_blocks, coef_index, owner_map):
     cosine = cosine_table()
     my_island = lax.axis_index("island")
     shard_rows = params.shape[0]
@@ -126,8 +132,16 @@
     previous = reduced[n_blocks : 2 * n_blocks]
     counts = reduced[2 * n_blocks :].reshape(-1)[:n_blocks]
 
-    rebuilt = decode(row_cos, col_cos, outgoing)
-    new_error = from_blocks(blocks - rebuilt, shard_rows, columns).astype(jnp.bfloat16)[None]
+    row_blocks = shard_rows // 64
+    err_chunks = ERR_CHUNKS if row_blocks % ERR_CHUNKS == 0 else 1
+    per = n_blocks // err_chunks
+    error_parts = []
+    for c in range(err_chunks):
+        part = slice(c * per, (c + 1) * per)
+        rebuilt = decode(row_cos[part], col_cos[part], outgoing[part])
+        fresh = from_blocks(blocks[part] - rebuilt, shard_rows // err_chunks, columns)
+        error_parts.append(fresh.astype(jnp.bfloat16))
+    new_error = jnp.concatenate(error_parts, axis=0)[None]
 
     average = totals / jnp.maximum(counts, 1.0)[:, None]
     refreshed = BETA_FACTOR * previous + average
@@ -138,11 +152,18 @@
     kept = BETA_FACTOR * mine
     new_momentum = jnp.where(owned_live[:, None], owned_fresh, kept).reshape(1, capacity * coef_total)
 
-    update = decode(row_cos, col_cos, update_coef).astype(jnp.bfloat16).astype(jnp.float32)
-    local_square = jnp.sum(update * update)
+    local_square = jnp.sum(update_coef * update_coef)
     total_square = butterfly_sum(local_square, "fsdp", fsdp_radices)
     scale_root = jnp.sqrt(total_square / (shard_rows * lax.axis_size("fsdp") * columns) + EPSILON)
-    shifted = from_blocks(update, shard_rows, columns)
+
+    upd_chunks = UPD_CHUNKS if row_blocks % UPD_CHUNKS == 0 else 1
+    per = n_blocks // upd_chunks
+    update_parts = []
+    for c in range(upd_chunks):
+        part = slice(c * per, (c + 1) * per)
+        update = decode(row_cos[part], col_cos[part], update_coef[part]).astype(jnp.bfloat16)
+        update_parts.append(from_blocks(update, shard_rows // upd_chunks, columns))
+    shifted = jnp.concatenate(update_parts, axis=0).astype(jnp.float32)
     new_params = (params.astype(jnp.float32) - OUTER_RATE * shifted / scale_root).astype(
         jnp.bfloat16
     )

time: 193 us -> 227 us (1.18)
  the two profiles are of different devices: /device:TPU:192 before, /device:TPU:16 now
where the time goes in v2:
time: 227 us; the launch traced here: 223 us
  local copies, waits for them, and re-layouts  90.2 us (40%)
  starting transfers between devices  48.4 us (21%)
  matrix products  36.7 us (16%)
  waiting for transfers between devices  23.7 us (10%)
  other arithmetic  19.7 us (9%)
  between operations  4.14 us (2%)
    ppermute x10, starting transfers between devices, butterfly_sum(): pieces[shift] = lax.ppermute(value, axis, perm)  48.4 us
    ppermute x10, waiting for transfers between devices, butterfly_sum(): pieces[shift] = lax.ppermute(value, axis, perm)  23.7 us
    mul x6, local copies, waits for them, and re-layouts, decode(): row_cos * values[:, :, None]  21.4 us
    dot_general x6, matrix products, decode(): jnp.einsum('bkj,bkl->bjl', row_cos * values[:, :, None], col_cos, precisi...  20.7 us
    slice x10, local copies, waits for them, and re-layouts, step_body(): rebuilt = decode(row_cos[part], col_cos[part], outgoing[part])  18.7 us
    dot_general x1, matrix products, step_body(): half = jnp.einsum('bkj,bjl->bkl', row_cos, blocks, precision=precise_mode)  11.7 us
    convert_element_type x8, local copies, waits for them, and re-layouts, step_body(): error_parts.append(fresh.astype(jnp.bfloat16))  10.7 us
    slice x3, local copies, waits for them, and re-layouts, step_body(): col_cos[part]  10.3 us
  transfers between devices with their start and end apart: 10, of which 5 were waited for; matrix products, arithmetic and copies ran while one was open for 44% of the time, Pallas kernels for 0%

profile of v2, /device:TPU:16, one launch (start us, length us, event | category | flops | bytes accessed | tf_op | source)
XLA Modules:
  0.0 222.8 jit_solution(14453269125242579351)
XLA Ops:
  5.8 2.6 %fusion.1 = f32[128,64,64]{0,2,1:T(8,128)} fusion(s32[128,64]{0,1:T(8,128)S(1)} %get-tuple-element.27, f32[64]{0:T(128)S(1)} %get-tuple-element.30, f32[64]{0:T(128)S(1)} %get-tuple-element.29), kind=kOutput, calls=%fused_computation.13 | convolution fusion | flops 403189760 | bytes 2130432 | tf_op jit(solution)/shard_map/...t,tc->...c/dot_general | solution.py:45
  11.3 4.9 %add.101 = f32[16,64,8,64]{3,2,1,0:T(8,128)} reshape(f32[1,1024,512]{2,1,0:T(8,128)} %convert_add_fusion) | data formatting | bytes 4194304 | tf_op jit(solution)/shard_map/add | solution.py:107
  16.2 5.3 %copy.85 = f32[16,8,64,64]{2,3,1,0:T(8,128)} copy(f32[16,8,64,64]{3,1,2,0:T(8,128)} %bitcast.62) | data formatting | bytes 4194304 | tf_op jit(solution)/shard_map/transpose | solution.py:28
  21.5 4.5 %copy.86 = f32[128,64,64]{2,1,0:T(8,128)} copy(f32[128,64,64]{0,2,1:T(8,128)S(1)} %fusion) | data formatting | bytes 4194304 | tf_op jit(solution)/shard_map/...t,tc->...c/dot_general | solution.py:45
  26.1 5.6 %copy.87 = f32[128,64,64]{1,2,0:T(8,128)} copy(f32[128,64,64]{0,2,1:T(8,128)} %fusion.1) | data formatting | bytes 4194304 | tf_op jit(solution)/shard_map/...t,tc->...c/dot_general | solution.py:45
  31.7 11.7 %multiply_reduce_fusion = f32[128,64]{1,0:T(8,128)S(1)} fusion(f32[128,64,64]{1,2,0:T(8,128)} %copy.87, f32[128,64,64]{2,1,0:T(8,128)} %copy.86, f32[128,64,64]{1,2,0:T(8,128)} %bitcast.63), kind=kOutput, calls=%fused_computation.1 | convolution fusion | flops 403693568 | bytes 6324224 | tf_op jit(solution)/shard_map/bkj,bjl->bkl/dot_general | solution.py:111
  43.9 2.1 collective-permute-start
  47.6 2.7 %fusion.36 = (f32[64,64,64]{0,2,1:T(8,128)}, f32[64,64,64]{0,2,1:T(8,128)}) fusion(f32[128,64,64]{0,2,1:T(8,128)S(1)} %copy-done), kind=kLoop, calls=%fused_computation.79 | loop fusion | bytes 4194304 | tf_op jit(solution)/shard_map/slice | solution.py:164
  50.3 5.0 %fusion.35 = (f32[32,64,64]{0,2,1:T(8,128)}, f32[32,64,64]{0,2,1:T(8,128)}, f32[32,64,64]{0,2,1:T(8,128)}, f32[32,64,64]{0,2,1:T(8,128)}) fusion(f32[128,64,64]{0,2,1:T(8,128)S(1)} %copy-done), kind=kLoop, calls=%fused_computation.78 | loop fusion | bytes 4194304 | tf_op jit(solution)/shard_map/slice | solution.py:141
  55.2 2.1 fusion.34
  57.6 5.1 %slice_multiply_fusion.3 = (f32[32,64,64]{0,2,1:T(8,128)}, f32[32,64,64]{0,2,1:T(8,128)}, f32[32,64,64]{0,2,1:T(8,128)}, f32[32,64,64]{0,2,1:T(8,128)}) fusion(f32[128,64,64]{0,2,1:T(8,128)S(1)} %fusion, f32[32,64]{0,1:T(8,128)S(1)} %copy.97, f32[32,64]{0,1:T(8,128)S(1)} %copy.109, f32[32,64]{0,1:T(8,128)S(1)} %copy.105, f32[32,64]{0,1:T(8,128)S(1)} %copy.101), kind=kLoop, calls=%fused_computation.5 | loop fusion | flops 524288 | bytes 4227072 | tf_op jit(solution)/shard_map/mul | solution.py:49
  62.8 3.9 %copy.98 = f32[32,64,64]{1,2,0:T(8,128)} copy(f32[32,64,64]{0,2,1:T(8,128)} %get-tuple-element.13) | data formatting | bytes 1048576 | tf_op jit(solution)/shard_map/mul | solution.py:49
  66.7 2.9 %copy.110 = f32[32,64,64]{1,2,0:T(8,128)S(1)} copy(f32[32,64,64]{0,2,1:T(8,128)} %get-tuple-element.14) | data formatting | bytes 1048576 | tf_op jit(solution)/shard_map/mul | solution.py:49
  69.6 3.4 %copy.99 = f32[32,64,64]{2,1,0:T(8,128)} copy(f32[32,64,64]{0,2,1:T(8,128)} %get-tuple-element.9) | data formatting | bytes 1048576 | tf_op jit(solution)/shard_map/slice | solution.py:141
  73.0 3.4 %copy.111 = f32[32,64,64]{2,1,0:T(8,128)} copy(f32[32,64,64]{0,2,1:T(8,128)} %get-tuple-element.10) | data formatting | bytes 1048576 | tf_op jit(solution)/shard_map/slice | solution.py:141
  76.3 4.0 %fusion.2 = bf16[32,64,64]{2,1,0:T(8,128)(2,1)} fusion(f32[32,64,64]{2,1,0:T(8,128)} %bitcast.70, f32[32,64,64]{1,2,0:T(8,128)} %copy.98, f32[32,64,64]{2,1,0:T(8,128)} %copy.99), kind=kOutput, calls=%fused_computation.20 | convolution fusion | flops 100925440 | bytes 1835008 | tf_op jit(solution)/shard_map/bkj,bkl->bjl/dot_general | solution.py:49
  80.3 2.1 fusion.5
  82.4 3.2 %copy.106 = f32[32,64,64]{1,2,0:T(8,128)S(1)} copy(f32[32,64,64]{0,2,1:T(8,128)} %get-tuple-element.15) | data formatting | bytes 1048576 | tf_op jit(solution)/shard_map/mul | solution.py:49
  85.6 3.3 %copy.107 = f32[32,64,64]{2,1,0:T(8,128)} copy(f32[32,64,64]{0,2,1:T(8,128)} %get-tuple-element.11) | data formatting | bytes 1048576 | tf_op jit(solution)/shard_map/slice | solution.py:141
  88.9 4.3 %collective-permute-start.1 = (f32[258,64]{1,0:T(8,128)S(1)}, f32[258,64]{1,0:T(8,128)S(1)}, u32[]{:S(2)}, u32[]{:S(2)}) collective-permute-start(f32[258,64]{1,0:T(8,128)S(1)} %fusion.33), channel_id=1, source_target_pairs={{0,16},{8,24},{16,0},{24,8},{32,48},{40,56},{48,32},{56,40},{64,80... | collective-permute-start | bytes 198152 | tf_op jit(solution)/shard_map/ppermute | solution.py:64
  93.2 3.5 %fusion.4 = bf16[32,64,64]{2,1,0:T(8,128)(2,1)} fusion(f32[32,64,64]{2,1,0:T(8,128)} %bitcast.68, f32[32,64,64]{1,2,0:T(8,128)S(1)} %copy.106, f32[32,64,64]{2,1,0:T(8,128)} %copy.107), kind=kOutput, calls=%fused_computation.22 | convolution fusion | flops 100925440 | bytes 1835008 | tf_op jit(solution)/shard_map/bkj,bkl->bjl/dot_general | solution.py:49
  96.7 2.9 %copy.102 = f32[32,64,64]{1,2,0:T(8,128)S(1)} copy(f32[32,64,64]{0,2,1:T(8,128)} %get-tuple-element.16) | data formatting | bytes 1048576 | tf_op jit(solution)/shard_map/mul | solution.py:49
  99.7 3.3 %copy.103 = f32[32,64,64]{2,1,0:T(8,128)} copy(f32[32,64,64]{0,2,1:T(8,128)} %get-tuple-element.12) | data formatting | bytes 1048576 | tf_op jit(solution)/shard_map/slice | solution.py:141
  103.1 6.1 %collective-permute-start.2 = (f32[258,64]{1,0:T(8,128)S(1)}, f32[258,64]{1,0:T(8,128)S(1)}, u32[]{:S(2)}, u32[]{:S(2)}) collective-permute-start(f32[258,64]{1,0:T(8,128)S(1)} %add.107), channel_id=1, source_target_pairs={{0,32},{8,40},{16,48},{24,56},{32,0},{40,8},{48,16},{56,24},{64,96... | collective-permute-start | bytes 198152 | tf_op jit(solution)/shard_map/ppermute | solution.py:64
  109.2 3.5 %fusion.3 = bf16[32,64,64]{2,1,0:T(8,128)(2,1)} fusion(f32[32,64,64]{2,1,0:T(8,128)} %bitcast.67, f32[32,64,64]{1,2,0:T(8,128)S(1)} %copy.102, f32[32,64,64]{2,1,0:T(8,128)} %copy.103), kind=kOutput, calls=%fused_computation.21 | convolution fusion | flops 100925440 | bytes 1835008 | tf_op jit(solution)/shard_map/bkj,bkl->bjl/dot_general | solution.py:49
  112.7 3.1 %collective-permute-done.2 = f32[258,64]{1,0:T(8,128)S(1)} collective-permute-done((f32[258,64]{1,0:T(8,128)S(1)}, f32[258,64]{1,0:T(8,128)S(1)}, u32[]{:S(2)}, u32[]{:S(2)}) %collective-permute-start.2) | collective-permute-done | bytes 66080 | tf_op jit(solution)/shard_map/ppermute | solution.py:64
  115.8 10.6 %collective-permute-start.4 = (f32[258,64]{1,0:T(8,128)S(1)}, f32[258,64]{1,0:T(8,128)S(1)}, u32[]{:S(2)}, u32[]{:S(2)}) collective-permute-start(f32[258,64]{1,0:T(8,128)S(1)} %add.108), channel_id=1, source_target_pairs={{0,64},{8,72},{16,80},{24,88},{32,96},{40,104},{48,112},{56,120},{... | collective-permute-start | bytes 198152 | tf_op jit(solution)/shard_map/ppermute | solution.py:64
  126.4 3.7 %collective-permute-start.3 = (f32[258,64]{1,0:T(8,128)S(1)}, f32[258,64]{1,0:T(8,128)S(1)}, u32[]{:S(2)}, u32[]{:S(2)}) collective-permute-start(f32[258,64]{1,0:T(8,128)S(1)} %add.108), channel_id=1, source_target_pairs={{0,128},{8,136},{16,144},{24,152},{32,160},{40,168},{48,176},{56,1... | collective-permute-start | bytes 198152 | tf_op jit(solution)/shard_map/ppermute | solution.py:64
  130.3 7.0 %collective-permute-done.4 = f32[258,64]{1,0:T(8,128)S(1)} collective-permute-done((f32[258,64]{1,0:T(8,128)S(1)}, f32[258,64]{1,0:T(8,128)S(1)}, u32[]{:S(2)}, u32[]{:S(2)}) %collective-permute-start.4) | collective-permute-done | bytes 66080 | tf_op jit(solution)/shard_map/ppermute | solution.py:64
  137.3 7.8 %collective-permute-done.3 = f32[258,64]{1,0:T(8,128)S(1)} collective-permute-done((f32[258,64]{1,0:T(8,128)S(1)}, f32[258,64]{1,0:T(8,128)S(1)}, u32[]{:S(2)}, u32[]{:S(2)}) %collective-permute-start.3) | collective-permute-done | bytes 66080 | tf_op jit(solution)/shard_map/ppermute | solution.py:64
  145.1 3.4 %collective-permute-start.5 = (f32[258,64]{1,0:T(8,128)S(1)}, f32[258,64]{1,0:T(8,128)}, u32[]{:S(2)}, u32[]{:S(2)}) collective-permute-start(f32[258,64]{1,0:T(8,128)S(1)} %select_add_fusion), channel_id=1, source_target_pairs={{0,192},{8,200},{16,208},{24,216},{32,224},{40,232},{48,240},{56,2... | collective-permute-start | bytes 198152 | tf_op jit(solution)/shard_map/ppermute | solution.py:64
  148.6 2.2 copy.100
  153.3 2.2 convert_element_type.120
  156.6 2.1 convert_element_type.116
  160.3 4.6 %collective-permute-start.6 = (f32[258,64]{1,0:T(8,128)S(1)}, f32[258,64]{1,0:T(8,128)S(1)}, u32[]{:S(2)}, u32[]{:S(2)}) collective-permute-start(f32[258,64]{1,0:T(8,128)S(1)} %add.112), channel_id=1, source_target_pairs={{0,384},{8,392},{16,400},{24,408},{32,416},{40,424},{48,432},{56,4... | collective-permute-start | bytes 198152 | tf_op jit(solution)/shard_map/ppermute | solution.py:64
  164.9 2.1 maximum_bitcast_fusion
  167.0 3.8 %copy.91 = f32[64,64,64]{2,1,0:T(8,128)} copy(f32[64,64,64]{0,2,1:T(8,128)} %get-tuple-element.17) | data formatting | bytes 2097152 | tf_op jit(solution)/shard_map/slice | solution.py:164
  170.8 3.8 %copy.95 = f32[64,64,64]{2,1,0:T(8,128)} copy(f32[64,64,64]{0,2,1:T(8,128)} %get-tuple-element.18) | data formatting | bytes 2097152 | tf_op jit(solution)/shard_map/slice | solution.py:164
  176.4 3.7 %collective-permute-start.7 = (f32[]{:T(128)}, f32[]{:T(128)}, u32[]{:S(2)}, u32[]{:S(2)}) collective-permute-start(f32[]{:T(128)} %get-tuple-element.3), channel_id=1, source_target_pairs={{0,1},{1,0},{2,3},{3,2},{4,5},{5,4},{6,7},{7,6},{8,9},{9,8},{10,11... | collective-permute-start | bytes 20 | tf_op jit(solution)/shard_map/ppermute | solution.py:64
  180.2 3.0 %slice_multiply_fusion.5 = (f32[64,64,64]{0,2,1:T(8,128)}, f32[64,64,64]{0,2,1:T(8,128)}) fusion(f32[128,64,64]{0,2,1:T(8,128)S(1)} %fusion, f32[64,64]{0,1:T(8,128)S(1)} %copy.89, f32[64,64]{0,1:T(8,128)S(1)} %copy.93), kind=kLoop, calls=%fused_computation.7 | loop fusion | flops 524288 | bytes 4227072 | tf_op jit(solution)/shard_map/mul | solution.py:49
  183.2 4.2 %copy.90 = f32[64,64,64]{1,2,0:T(8,128)} copy(f32[64,64,64]{0,2,1:T(8,128)} %get-tuple-element.19) | data formatting | bytes 2097152 | tf_op jit(solution)/shard_map/mul | solution.py:49
  187.3 4.3 %copy.94 = f32[64,64,64]{1,2,0:T(8,128)} copy(f32[64,64,64]{0,2,1:T(8,128)} %get-tuple-element.20) | data formatting | bytes 2097152 | tf_op jit(solution)/shard_map/mul | solution.py:49
  191.6 3.8 %convolution_convert_fusion.1 = bf16[64,64,64]{2,1,0:T(8,128)(2,1)S(1)} fusion(f32[64,64,64]{1,2,0:T(8,128)} %copy.90, f32[64,64,64]{2,1,0:T(8,128)S(1)} %copy-done.3), kind=kOutput, calls=%fused_computation.15 | convolution fusion | flops 201588736 | bytes 2621440 | tf_op jit(solution)/shard_map/bkj,bkl->bjl/dot_general | solution.py:49
  197.6 3.8 %convolution_convert_fusion = bf16[64,64,64]{2,1,0:T(8,128)(2,1)S(1)} fusion(f32[64,64,64]{1,2,0:T(8,128)} %copy.94, f32[64,64,64]{2,1,0:T(8,128)S(1)} %copy-done.2), kind=kOutput, calls=%fused_computation.14 | convolution fusion | flops 201588736 | bytes 2621440 | tf_op jit(solution)/shard_map/bkj,bkl->bjl/dot_general | solution.py:49
  204.0 3.5 %collective-permute-start.8 = (f32[]{:T(128)}, f32[]{:T(128)}, u32[]{:S(2)}, u32[]{:S(2)}) collective-permute-start(f32[]{:T(128)} %add.116), channel_id=1, source_target_pairs={{0,2},{1,3},{2,0},{3,1},{4,6},{5,7},{6,4},{7,5},{8,10},{9,11},{10,... | collective-permute-start | bytes 20 | tf_op jit(solution)/shard_map/ppermute | solution.py:64
  207.5 2.8 %collective-permute-done.8 = f32[]{:T(128)} collective-permute-done((f32[]{:T(128)}, f32[]{:T(128)}, u32[]{:S(2)}, u32[]{:S(2)}) %collective-permute-start.8) | collective-permute-done | bytes 36 | tf_op jit(solution)/shard_map/ppermute | solution.py:64
  211.0 6.3 %collective-permute-start.9 = (f32[]{:T(128)}, f32[]{:T(128)}, u32[]{:S(2)}, u32[]{:S(2)}) collective-permute-start(f32[]{:T(128)} %add.117), channel_id=1, source_target_pairs={{0,4},{1,5},{2,6},{3,7},{4,0},{5,1},{6,2},{7,3},{8,12},{9,13},{10,... | collective-permute-start | bytes 20 | tf_op jit(solution)/shard_map/ppermute | solution.py:64
  217.3 3.0 %collective-permute-done.9 = f32[]{:T(128)} collective-permute-done((f32[]{:T(128)}, f32[]{:T(128)}, u32[]{:S(2)}, u32[]{:S(2)}) %collective-permute-start.9) | collective-permute-done | bytes 36 | tf_op jit(solution)/shard_map/ppermute | solution.py:64
  (91 shorter events, 22.5 us)
Async XLA Ops:
  0.7 42.8 %copy-start.15 = (s32[2]{0:T(128)}, s32[2]{0:T(128)S(1)}, u32[]{:S(2)}) copy-start(s32[2]{0:T(128)S(1)} %iota_add_fusion) | copy-start | bytes 28
  2.6 40.9 %copy-start.13 = (f32[2,64]{1,0:T(2,128)}, f32[2,64]{1,0:T(2,128)S(1)}, u32[]{:S(2)}) copy-start(f32[2,64]{1,0:T(2,128)S(1)} %reshape_squeeze.3) | copy-start | bytes 1540
  4.9 38.6 %copy-start.17 = (s32[128]{0:T(128)}, s32[128]{0:T(128)S(1)}, u32[]{:S(2)}) copy-start(s32[128]{0:T(128)S(1)} %multiply_add_fusion.1) | copy-start | bytes 1540
  5.8 3.8 %copy-start.11 = (bf16[1,1024,512]{2,1,0:T(8,128)(2,1)S(1)}, bf16[1,1024,512]{2,1,0:T(8,128)(2,1)}, u32[]{:S(2)}) copy-start(bf16[1,1024,512]{2,1,0:T(8,128)(2,1)} %param.8) | copy-start | bytes 3145732
  5.8 3.8 %copy-start.12 = (bf16[1,1024,512]{2,1,0:T(8,128)(2,1)S(1)}, bf16[1,1024,512]{2,1,0:T(8,128)(2,1)}, u32[]{:S(2)}) copy-start(bf16[1,1024,512]{2,1,0:T(8,128)(2,1)} %param.7) | copy-start | bytes 3145732
  31.7 14.2 %copy-start.1 = (f32[16,64,8,64]{3,2,1,0:T(8,128)S(1)}, f32[16,64,8,64]{3,2,1,0:T(8,128)}, u32[]{:S(2)}) copy-start(f32[16,64,8,64]{3,2,1,0:T(8,128)} %add.101) | copy-start | bytes 6291460
  43.9 45.1 %collective-permute-start = (f32[258,64]{1,0:T(8,128)S(1)}, f32[258,64]{1,0:T(8,128)S(1)}, u32[]{:S(2)}, u32[]{:S(2)}) collective-permute-start(f32[258,64]{1,0:T(8,128)S(1)} %pad_maximum_fusion), channel_id=1, source_target_pairs={{0,8},{8,0},{16,24},{24,16},{32,40},{40,32},{48,56},{56,48},{64,72... | collective-permute-start | bytes 198152 | tf_op jit(solution)/shard_map/ppermute | solution.py:64
  46.0 1.6 copy-start
  76.3 4.0 %copy-start.4 = (f32[32,64,64]{2,1,0:T(8,128)S(1)}, f32[32,64,64]{2,1,0:T(8,128)}, u32[]{:S(2)}) copy-start(f32[32,64,64]{2,1,0:T(8,128)} %copy.111) | copy-start | bytes 1572868
  76.3 4.0 %copy-start.5 = (f32[4,8,64,64]{3,2,1,0:T(8,128)S(1)}, f32[4,8,64,64]{3,2,1,0:T(8,128)}, u32[]{:S(2)}) copy-start(f32[4,8,64,64]{3,2,1,0:T(8,128)} %get-tuple-element.8) | copy-start | bytes 1572868
  88.9 14.1 %collective-permute-start.1 = (f32[258,64]{1,0:T(8,128)S(1)}, f32[258,64]{1,0:T(8,128)S(1)}, u32[]{:S(2)}, u32[]{:S(2)}) collective-permute-start(f32[258,64]{1,0:T(8,128)S(1)} %fusion.33), channel_id=1, source_target_pairs={{0,16},{8,24},{16,0},{24,8},{32,48},{40,56},{48,32},{56,40},{64,80... | collective-permute-start | bytes 198152 | tf_op jit(solution)/shard_map/ppermute | solution.py:64
  103.1 27.0 %copy-start.16 = (s32[2]{0:T(128)S(1)}, s32[2]{0:T(128)}, u32[]{:S(2)}) copy-start(s32[2]{0:T(128)} %copy-done.15) | copy-start | bytes 28
  103.1 27.0 %copy-start.18 = (s32[128]{0:T(128)S(1)}, s32[128]{0:T(128)}, u32[]{:S(2)}) copy-start(s32[128]{0:T(128)} %copy-done.17) | copy-start | bytes 1540
  103.1 12.7 %collective-permute-start.2 = (f32[258,64]{1,0:T(8,128)S(1)}, f32[258,64]{1,0:T(8,128)S(1)}, u32[]{:S(2)}, u32[]{:S(2)}) collective-permute-start(f32[258,64]{1,0:T(8,128)S(1)} %add.107), channel_id=1, source_target_pairs={{0,32},{8,40},{16,48},{24,56},{32,0},{40,8},{48,16},{56,24},{64,96... | collective-permute-start | bytes 198152 | tf_op jit(solution)/shard_map/ppermute | solution.py:64
  112.7 39.4 %copy-start.6 = (bf16[32,64,64]{2,1,0:T(8,128)(2,1)S(1)}, bf16[32,64,64]{2,1,0:T(8,128)(2,1)}, u32[]{:S(2)}) copy-start(bf16[32,64,64]{2,1,0:T(8,128)(2,1)} %fusion.5) | copy-start | bytes 786436
  115.8 21.6 %collective-permute-start.4 = (f32[258,64]{1,0:T(8,128)S(1)}, f32[258,64]{1,0:T(8,128)S(1)}, u32[]{:S(2)}, u32[]{:S(2)}) collective-permute-start(f32[258,64]{1,0:T(8,128)S(1)} %add.108), channel_id=1, source_target_pairs={{0,64},{8,72},{16,80},{24,88},{32,96},{40,104},{48,112},{56,120},{... | collective-permute-start | bytes 198152 | tf_op jit(solution)/shard_map/ppermute | solution.py:64
  126.4 18.7 %collective-permute-start.3 = (f32[258,64]{1,0:T(8,128)S(1)}, f32[258,64]{1,0:T(8,128)S(1)}, u32[]{:S(2)}, u32[]{:S(2)}) collective-permute-start(f32[258,64]{1,0:T(8,128)S(1)} %add.108), channel_id=1, source_target_pairs={{0,128},{8,136},{16,144},{24,152},{32,160},{40,168},{48,176},{56,1... | collective-permute-start | bytes 198152 | tf_op jit(solution)/shard_map/ppermute | solution.py:64
  130.3 25.1 %copy-start.7 = (bf16[32,64,64]{2,1,0:T(8,128)(2,1)S(1)}, bf16[32,64,64]{2,1,0:T(8,128)(2,1)}, u32[]{:S(2)}) copy-start(bf16[32,64,64]{2,1,0:T(8,128)(2,1)} %fusion.4) | copy-start | bytes 786436
  145.1 14.2 %collective-permute-start.5 = (f32[258,64]{1,0:T(8,128)S(1)}, f32[258,64]{1,0:T(8,128)}, u32[]{:S(2)}, u32[]{:S(2)}) collective-permute-start(f32[258,64]{1,0:T(8,128)S(1)} %select_add_fusion), channel_id=1, source_target_pairs={{0,192},{8,200},{16,208},{24,216},{32,224},{40,232},{48,240},{56,2... | collective-permute-start | bytes 198152 | tf_op jit(solution)/shard_map/ppermute | solution.py:64
  153.3 5.4 %copy-start.8 = (bf16[32,64,64]{2,1,0:T(8,128)(2,1)S(1)}, bf16[32,64,64]{2,1,0:T(8,128)(2,1)}, u32[]{:S(2)}) copy-start(bf16[32,64,64]{2,1,0:T(8,128)(2,1)} %fusion.3) | copy-start | bytes 786436
  160.3 14.3 %collective-permute-start.6 = (f32[258,64]{1,0:T(8,128)S(1)}, f32[258,64]{1,0:T(8,128)S(1)}, u32[]{:S(2)}, u32[]{:S(2)}) collective-permute-start(f32[258,64]{1,0:T(8,128)S(1)} %add.112), channel_id=1, source_target_pairs={{0,384},{8,392},{16,400},{24,408},{32,416},{40,424},{48,432},{56,4... | collective-permute-start | bytes 198152 | tf_op jit(solution)/shard_map/ppermute | solution.py:64
  170.8 4.7 %copy-start.14 = (f32[2,64]{1,0:T(2,128)S(1)}, f32[2,64]{1,0:T(2,128)}, u32[]{:S(2)}) copy-start(f32[2,64]{1,0:T(2,128)} %copy-done.13) | copy-start | bytes 1540
  176.4 26.3 %collective-permute-start.7 = (f32[]{:T(128)}, f32[]{:T(128)}, u32[]{:S(2)}, u32[]{:S(2)}) collective-permute-start(f32[]{:T(128)} %get-tuple-element.3), channel_id=1, source_target_pairs={{0,1},{1,0},{2,3},{3,2},{4,5},{5,4},{6,7},{7,6},{8,9},{9,8},{10,11... | collective-permute-start | bytes 20 | tf_op jit(solution)/shard_map/ppermute | solution.py:64
  187.3 4.3 %copy-start.3 = (f32[64,64,64]{2,1,0:T(8,128)S(1)}, f32[64,64,64]{2,1,0:T(8,128)}, u32[]{:S(2)}) copy-start(f32[64,64,64]{2,1,0:T(8,128)} %copy.91) | copy-start | bytes 3145732
  195.4 2.1 copy-start.2
  201.4 19.6 %copy-start.9 = (bf16[512,512]{1,0:T(8,128)(2,1)S(1)}, bf16[512,512]{1,0:T(8,128)(2,1)}, u32[]{:S(2)}) copy-start(bf16[512,512]{1,0:T(8,128)(2,1)} %reshape.102) | copy-start | bytes 1572868
  201.4 19.6 %copy-start.10 = (bf16[1024,512]{1,0:T(8,128)(2,1)S(1)}, bf16[1024,512]{1,0:T(8,128)(2,1)}, u32[]{:S(2)}) copy-start(bf16[1024,512]{1,0:T(8,128)(2,1)} %param.9) | copy-start | bytes 3145732
  204.0 6.3 %collective-permute-start.8 = (f32[]{:T(128)}, f32[]{:T(128)}, u32[]{:S(2)}, u32[]{:S(2)}) collective-permute-start(f32[]{:T(128)} %add.116), channel_id=1, source_target_pairs={{0,2},{1,3},{2,0},{3,1},{4,6},{5,7},{6,4},{7,5},{8,10},{9,11},{10,... | collective-permute-start | bytes 20 | tf_op jit(solution)/shard_map/ppermute | solution.py:64
  211.0 9.3 %collective-permute-start.9 = (f32[]{:T(128)}, f32[]{:T(128)}, u32[]{:S(2)}, u32[]{:S(2)}) collective-permute-start(f32[]{:T(128)} %add.117), channel_id=1, source_target_pairs={{0,4},{1,5},{2,6},{3,7},{4,0},{5,1},{6,2},{7,3},{8,12},{9,13},{10,... | collective-permute-start | bytes 20 | tf_op jit(solution)/shard_map/ppermute | solution.py:64

commit v3 on v1

--- a/solution.py
+++ b/solution.py
@@ -4,6 +4,8 @@
 import jax.numpy as jnp
 from jax import lax
 from jax.sharding import PartitionSpec as P
+from jax.experimental import pallas as pl
+from jax.experimental.pallas import tpu as pltpu
 
 BETA_FACTOR = 0.9
 OUTER_RATE = 0.5
@@ -47,10 +49,11 @@
     return jnp.einsum("bkj,bkl->bjl", row_cos * values[:, :, None], col_cos, precision=precise_mode)
 
 
-def butterfly_sum(value, axis, radices):
+def butterfly_sum(value, axis, radices, tag):
     size = lax.axis_size(axis)
     here = lax.axis_index(axis)
     stride = 1
+    done_rounds = []
     for radix in radices:
         digit = (here // stride) % radix
         pieces = {0: value}
@@ -59,7 +62,8 @@
             for src in range(size):
                 d = (src // stride) % radix
                 perm.append((src, src + ((d + shift) % radix - d) * stride))
-            pieces[shift] = lax.ppermute(value, axis, perm)
+            with jax.named_scope(f"{tag}{len(done_rounds)}s{shift}"):
+                pieces[shift] = lax.ppermute(value, axis, perm)
         if radix == 2:
             value = pieces[0] + pieces[1]
         else:
@@ -73,6 +77,7 @@
             for e in range(1, radix):
                 value = value + ordered[e]
         stride *= radix
+        done_rounds.append(radix)
     return value
 
 
@@ -89,26 +94,103 @@
     return out
 
 
+def _rows(idx_col, cos):
+    hot = (idx_col == lax.broadcasted_iota(jnp.int32, (idx_col.shape[0], 64), 1)).astype(jnp.float32)
+    return jnp.dot(hot, cos, precision=precise_mode, preferred_element_type=jnp.float32)
+
+
+def _encode_kernel(cos_ref, idx_ref, mask_ref, g_ref, e_ref, sent_ref, err_ref):
+    cos = cos_ref[...]
+    for cb in range(idx_ref.shape[2]):
+        cols = slice(cb * 64, (cb + 1) * 64)
+        idx = idx_ref[0, :, cb : cb + 1]
+        row_cos = _rows(idx // 64, cos)
+        col_cos = _rows(idx % 64, cos)
+        x = g_ref[:, cols].astype(jnp.float32) + e_ref[:, cols].astype(jnp.float32)
+        half = jnp.dot(row_cos, x, precision=precise_mode, preferred_element_type=jnp.float32)
+        sent = jnp.sum(half * col_cos, axis=1, keepdims=True) * mask_ref[0, :, cb : cb + 1]
+        sent_ref[0, :, cb : cb + 1] = sent
+        rebuilt = jnp.dot((row_cos * sent).T, col_cos, precision=precise_mode, preferred_element_type=jnp.float32)
+        err_ref[:, cols] = (x - rebuilt).astype(err_ref.dtype)
+
+
+def encode(grad, error, idx_t3, mask3):
+    rows, columns = grad.shape
+    row_blocks = rows // 64
+    col_blocks = columns // 64
+    return pl.pallas_call(
+        _encode_kernel,
+        grid=(row_blocks,),
+        in_specs=[
+            pl.BlockSpec((64, 64), lambda i: (0, 0)),
+            pl.BlockSpec((1, 64, col_blocks), lambda i: (i, 0, 0)),
+            pl.BlockSpec((1, 1, col_blocks), lambda i: (i, 0, 0)),
+            pl.BlockSpec((64, columns), lambda i: (i, 0)),
+            pl.BlockSpec((64, columns), lambda i: (i, 0)),
+        ],
+        out_specs=[
+            pl.BlockSpec((1, 64, col_blocks), lambda i: (i, 0, 0)),
+            pl.BlockSpec((64, columns), lambda i: (i, 0)),
+        ],
+        out_shape=[
+            jax.ShapeDtypeStruct((row_blocks, 64, col_blocks), jnp.float32),
+            jax.ShapeDtypeStruct((rows, columns), jnp.bfloat16),
+        ],
+        compiler_params=pltpu.CompilerParams(dimension_semantics=("parallel",)),
+    )(cosine_table(), idx_t3, mask3, grad, error)
+
+
+def _apply_kernel(rate, cos_ref, idx_ref, coef_ref, scale_ref, p_ref, out_ref):
+    cos = cos_ref[...]
+    scale = scale_ref[0, 0]
+    for cb in range(idx_ref.shape[2]):
+        cols = slice(cb * 64, (cb + 1) * 64)
+        idx = idx_ref[0, :, cb : cb + 1]
+        row_cos = _rows(idx // 64, cos)
+        col_cos = _rows(idx % 64, cos)
+        coef = coef_ref[0, :, cb : cb + 1]
+        update = jnp.dot((row_cos * coef).T, col_cos, precision=precise_mode, preferred_element_type=jnp.float32)
+        update = update.astype(jnp.bfloat16).astype(jnp.float32)
+        out_ref[:, cols] = (p_ref[:, cols].astype(jnp.float32) - rate * update / scale).astype(out_ref.dtype)
+
+
+def apply_update(params, idx_t3, coef3, scale, rate):
+    rows, columns = params.shape
+    row_blocks = rows // 64
+    col_blocks = columns // 64
+    return pl.pallas_call(
+        functools.partial(_apply_kernel, rate),
+        grid=(row_blocks,),
+        in_specs=[
+            pl.BlockSpec((64, 64), lambda i: (0, 0)),
+            pl.BlockSpec((1, 64, col_blocks), lambda i: (i, 0, 0)),
+            pl.BlockSpec((1, 64, col_blocks), lambda i: (i, 0, 0)),
+            pl.BlockSpec(memory_space=pltpu.SMEM),
+            pl.BlockSpec((64, columns), lambda i: (i, 0)),
+        ],
+        out_specs=pl.BlockSpec((64, columns), lambda i: (i, 0)),
+        out_shape=jax.ShapeDtypeStruct((rows, columns), jnp.bfloat16),
+        compiler_params=pltpu.CompilerParams(dimension_semantics=("parallel",)),
+    )(cosine_table(), idx_t3, coef3, scale.reshape(1, 1), params)
+
+
 def on_device(island_radices, fsdp_radices, pseudo_grad, error_buf, params, momentum, sel_blocks, coef_index, owner_map):
-    cosine = cosine_table()
     my_island = lax.axis_index("island")
     shard_rows = params.shape[0]
     columns = params.shape[1]
     n_blocks = coef_index.shape[0]
     coef_total = coef_index.shape[1]
     capacity = momentum.shape[1] // coef_total
-
-    summed = pseudo_grad[0].astype(jnp.float32) + error_buf[0].astype(jnp.float32)
-    blocks = to_blocks(summed)
-    row_cos = one_hot_rows(cosine, coef_index // 64)
-    col_cos = one_hot_rows(cosine, coef_index % 64)
-    half = jnp.einsum("bkj,bjl->bkl", row_cos, blocks, precision=precise_mode)
-    picked = jnp.sum(half * col_cos, axis=2)
+    row_blocks = shard_rows // 64
+    col_blocks = columns // 64
 
     chosen = sel_blocks[0]
     block_ids = jnp.arange(n_blocks, dtype=jnp.int32)
     chosen_mask = jnp.any(chosen[:, None] == block_ids[None, :], axis=0).astype(jnp.float32)
-    outgoing = picked * chosen_mask[:, None]
+    idx_t3 = coef_index.reshape(row_blocks, col_blocks, coef_total).transpose(0, 2, 1)
+    sent3, fresh_error = encode(pseudo_grad[0], error_buf[0], idx_t3, chosen_mask.reshape(row_blocks, 1, col_blocks))
+    new_error = fresh_error[None]
+    outgoing = sent3.transpose(0, 2, 1).reshape(n_blocks, coef_total)
 
     earlier = (owner_map[None, :] == owner_map[:, None]) & (block_ids[None, :] < block_ids[:, None])
     slot_of = jnp.sum(earlier.astype(jnp.int32), axis=1)
@@ -121,13 +203,10 @@
     mask_rows = -(-n_blocks // coef_total)
     mask_part = jnp.pad(chosen_mask, (0, mask_rows * coef_total - n_blocks)).reshape(mask_rows, coef_total)
     payload = jnp.concatenate([outgoing, held, mask_part], axis=0)
-    reduced = butterfly_sum(payload, "island", island_radices)
+    reduced = butterfly_sum(payload, "island", island_radices, "isl")
     totals = reduced[:n_blocks]
     previous = reduced[n_blocks : 2 * n_blocks]
     counts = reduced[2 * n_blocks :].reshape(-1)[:n_blocks]
-
-    rebuilt = decode(row_cos, col_cos, outgoing)
-    new_error = from_blocks(blocks - rebuilt, shard_rows, columns).astype(jnp.bfloat16)[None]
 
     average = totals / jnp.maximum(counts, 1.0)[:, None]
     refreshed = BETA_FACTOR * previous + average
@@ -138,14 +217,12 @@
     kept = BETA_FACTOR * mine
     new_momentum = jnp.where(owned_live[:, None], owned_fresh, kept).reshape(1, capacity * coef_total)
 
-    update = decode(row_cos, col_cos, update_coef).astype(jnp.bfloat16).astype(jnp.float32)
-    local_square = jnp.sum(update * update)
-    total_square = butterfly_sum(local_square, "fsdp", fsdp_radices)
+    local_square = jnp.sum(update_coef * update_coef)
+    total_square = butterfly_sum(local_square, "fsdp", fsdp_radices, "fsd")
     scale_root = jnp.sqrt(total_square / (shard_rows * lax.axis_size("fsdp") * columns) + EPSILON)
-    shifted = from_blocks(update, shard_rows, columns)
-    new_params = (params.astype(jnp.float32) - OUTER_RATE * shifted / scale_root).astype(
-        jnp.bfloat16
-    )
+
+    coef3 = update_coef.reshape(row_blocks, col_blocks, coef_total).transpose(0, 2, 1)
+    new_params = apply_update(params, idx_t3, coef3, scale_root, OUTER_RATE)
     return (new_params, new_error, new_momentum)
 
 

time: 193 us -> 201 us (1.041); the launches traced: 190 us -> 200 us
  Pallas kernels: 0 us -> 100 us
  local copies, waits for them, and re-layouts: 47.4 us -> 5.98 us
  matrix products: 38.4 us -> 0.53 us
  other arithmetic: 12.5 us -> 4.06 us
    pallas_call x0 -> x2, Pallas kernels: none -> 100 us  [the longest x1 65 us: encode(): pl.pallas_call(_encode_kernel, grid=(row_blocks,), in_specs=[pl.BlockSpec...]
    dot_general x5 -> x0, matrix products: 37.8 us -> none  [the longest x2 22.4 us: decode(): jnp.einsum('bkj,bkl->bjl', row_cos * values[:, :, None], col_cos, precisi...]
    dot_general x2 -> x0, local copies, waits for them, and re-layouts: 10.4 us -> none  [one_hot_rows(): return jnp.einsum('...t,tc->...c', hot, table, precision=precise_mode)]
    mul x3 -> x0, local copies, waits for them, and re-layouts: 10.4 us -> none  [the longest x2 10.3 us: decode(): row_cos * values[:, :, None]]
    add x3 -> x0, local copies, waits for them, and re-layouts: 9.36 us -> none  [the longest x2 9.27 us: on_device(): pseudo_grad[0].astype(jnp.float32) + error_buf[0].astype(jnp.float32)]
    div x2 -> x0, local copies, waits for them, and re-layouts: 8.72 us -> none  [on_device(): OUTER_RATE * shifted / scale_root]
    convert_element_type x2 -> x0, local copies, waits for them, and re-layouts: 7.19 us -> none  [on_device(): from_blocks(blocks - rebuilt, shard_rows, columns).astype(jnp.bfloat16)]
    add x2 -> x0, other arithmetic: 2.95 us -> none  [the longest x1 2.86 us: on_device(): pseudo_grad[0].astype(jnp.float32) + error_buf[0].astype(jnp.float32)]
  transfers between devices with their start and end apart: 10 -> 10, of which waited for: 10 -> 10; matrix products, arithmetic and copies ran while one was open for 0% -> 1% of each run, Pallas kernels for 0% -> 0%
where the time goes in v3:
time: 201 us; the launch traced here: 200 us
  Pallas kernels  100 us (50%)
  starting transfers between devices  46.9 us (23%)
  waiting for transfers between devices  39.2 us (20%)
  local copies, waits for them, and re-layouts  5.98 us (3%)
  other arithmetic  4.06 us (2%)
  between operations  3.45 us (2%)
    pallas_call x1, Pallas kernels, encode(): pl.pallas_call(_encode_kernel, grid=(row_blocks,), in_specs=[pl.BlockSpec...  65 us
    ppermute x10, starting transfers between devices, butterfly_sum(): pieces[shift] = lax.ppermute(value, axis, perm)  46.9 us
    ppermute x10, waiting for transfers between devices, butterfly_sum(): pieces[shift] = lax.ppermute(value, axis, perm)  39.2 us
    pallas_call x1, Pallas kernels, apply_update(): pl.pallas_call(functools.partial(_apply_kernel, rate), grid=(row_blocks,)...  35.3 us
  transfers between devices with their start and end apart: 10, of which 10 were waited for; matrix products, arithmetic and copies ran while one was open for 1% of the time, Pallas kernels for 0%

profile of v3, /device:TPU:192, one launch (start us, length us, event | category | flops | bytes accessed | tf_op | source)
XLA Modules:
  0.0 200.4 jit_solution(15218600175127794025)
XLA Ops:
  0.6 0.0 copy-start
  0.7 0.7 fusion.3
  1.4 0.1 reshape.79
  1.5 0.7 reshape.78
  2.2 0.5 broadcast.95
  2.7 1.3 reduce.3
  4.0 0.0 copy-start.1
  4.0 0.1 reshape_squeeze.3
  4.1 0.6 copy-done.1
  4.7 0.2 convert_reduce_fusion
  4.9 0.0 copy-done
  4.9 0.1 copy.31
  5.0 1.0 copy.32
  6.0 0.8 cosine_multiply_fusion.cos_ref
  6.7 65.0 %shard_map.94 = (f32[16,64,8]{2,1,0:T(8,128)}, bf16[1024,512]{1,0:T(8,128)(2,1)}) custom-call(f32[64,64]{1,0:T(8,128)} %cosine_multiply_fusion.cos_ref, s32[16,64,8]{2,1,0:T(8,128)} %bitcast.14, f32[16,1,8]{2,1,0:T(1,128)} %bitcast.23, bf16[1024,512]{1,0:T(8,128)(2,1)} %bitcast.17, bf16[1024,512]{1,0:T(8,128)(2,1)} %bitcast.18), custom_call_target="tpu_custom_call" | custom-call | tf_op jit(solution)/shard_map/pallas_call | solution.py:121
  71.7 1.2 copy.34
  73.0 0.3 fusion.6
  73.3 1.9 collective-permute-start
  75.2 1.3 collective-permute-done
  76.6 1.9 collective-permute-start.1
  78.5 5.6 %collective-permute-done.1 = f32[258,64]{1,0:T(8,128)S(1)} collective-permute-done((f32[258,64]{1,0:T(8,128)S(1)}, f32[258,64]{1,0:T(8,128)S(1)}, u32[]{:S(2)}, u32[]{:S(2)}) %collective-permute-start.1) | collective-permute-done | bytes 66080 | tf_op jit(solution)/shard_map/isl1s1/ppermute | solution.py:66
  84.1 7.6 %collective-permute-start.2 = (f32[258,64]{1,0:T(8,128)S(1)}, f32[258,64]{1,0:T(8,128)S(1)}, u32[]{:S(2)}, u32[]{:S(2)}) collective-permute-start(f32[258,64]{1,0:T(8,128)S(1)} %add.87), channel_id=1, source_target_pairs={{0,32},{8,40},{16,48},{24,56},{32,0},{40,8},{48,16},{56,24},{64,96... | collective-permute-start | bytes 198152 | tf_op jit(solution)/shard_map/isl2s1/ppermute | solution.py:66
  91.7 6.2 %collective-permute-done.2 = f32[258,64]{1,0:T(8,128)S(1)} collective-permute-done((f32[258,64]{1,0:T(8,128)S(1)}, f32[258,64]{1,0:T(8,128)S(1)}, u32[]{:S(2)}, u32[]{:S(2)}) %collective-permute-start.2) | collective-permute-done | bytes 66080 | tf_op jit(solution)/shard_map/isl2s1/ppermute | solution.py:66
  97.9 7.3 %collective-permute-start.4 = (f32[258,64]{1,0:T(8,128)S(1)}, f32[258,64]{1,0:T(8,128)S(1)}, u32[]{:S(2)}, u32[]{:S(2)}) collective-permute-start(f32[258,64]{1,0:T(8,128)S(1)} %add.88), channel_id=1, source_target_pairs={{0,64},{8,72},{16,80},{24,88},{32,96},{40,104},{48,112},{56,120},{... | collective-permute-start | bytes 198152 | tf_op jit(solution)/shard_map/isl3s1/ppermute | solution.py:66
  105.3 3.1 %collective-permute-start.3 = (f32[258,64]{1,0:T(8,128)S(1)}, f32[258,64]{1,0:T(8,128)S(1)}, u32[]{:S(2)}, u32[]{:S(2)}) collective-permute-start(f32[258,64]{1,0:T(8,128)S(1)} %add.88), channel_id=1, source_target_pairs={{0,128},{8,136},{16,144},{24,152},{32,160},{40,168},{48,176},{56,1... | collective-permute-start | bytes 198152 | tf_op jit(solution)/shard_map/isl3s2/ppermute | solution.py:66
  108.5 8.4 %collective-permute-done.4 = f32[258,64]{1,0:T(8,128)S(1)} collective-permute-done((f32[258,64]{1,0:T(8,128)S(1)}, f32[258,64]{1,0:T(8,128)S(1)}, u32[]{:S(2)}, u32[]{:S(2)}) %collective-permute-start.4) | collective-permute-done | bytes 66080 | tf_op jit(solution)/shard_map/isl3s1/ppermute | solution.py:66
  116.9 6.9 %collective-permute-done.3 = f32[258,64]{1,0:T(8,128)S(1)} collective-permute-done((f32[258,64]{1,0:T(8,128)S(1)}, f32[258,64]{1,0:T(8,128)S(1)}, u32[]{:S(2)}, u32[]{:S(2)}) %collective-permute-start.3) | collective-permute-done | bytes 66080 | tf_op jit(solution)/shard_map/isl3s2/ppermute | solution.py:66
  123.8 3.1 %collective-permute-start.5 = (f32[258,64]{1,0:T(8,128)S(1)}, f32[258,64]{1,0:T(8,128)S(1)}, u32[]{:S(2)}, u32[]{:S(2)}) collective-permute-start(f32[258,64]{1,0:T(8,128)S(1)} %select_add_fusion), channel_id=1, source_target_pairs={{0,192},{8,200},{16,208},{24,216},{32,224},{40,232},{48,240},{56,2... | collective-permute-start | bytes 198152 | tf_op jit(solution)/shard_map/isl4s1/ppermute | solution.py:66
  126.9 0.2 fusion.8
  127.1 4.1 %collective-permute-done.5 = f32[258,64]{1,0:T(8,128)S(1)} collective-permute-done((f32[258,64]{1,0:T(8,128)S(1)}, f32[258,64]{1,0:T(8,128)S(1)}, u32[]{:S(2)}, u32[]{:S(2)}) %collective-permute-start.5) | collective-permute-done | bytes 66080 | tf_op jit(solution)/shard_map/isl4s1/ppermute | solution.py:66
  131.3 4.6 %collective-permute-start.6 = (f32[258,64]{1,0:T(8,128)S(1)}, f32[258,64]{1,0:T(8,128)S(1)}, u32[]{:S(2)}, u32[]{:S(2)}) collective-permute-start(f32[258,64]{1,0:T(8,128)S(1)} %add.92), channel_id=1, source_target_pairs={{0,384},{8,392},{16,400},{24,408},{32,416},{40,424},{48,432},{56,4... | collective-permute-start | bytes 198152 | tf_op jit(solution)/shard_map/isl5s1/ppermute | solution.py:66
  135.9 3.8 %collective-permute-done.6 = f32[258,64]{1,0:T(8,128)S(1)} collective-permute-done((f32[258,64]{1,0:T(8,128)S(1)}, f32[258,64]{1,0:T(8,128)S(1)}, u32[]{:S(2)}, u32[]{:S(2)}) %collective-permute-start.6) | collective-permute-done | bytes 66080 | tf_op jit(solution)/shard_map/isl5s1/ppermute | solution.py:66
  139.7 0.1 max.15
  139.8 0.7 multiply_reduce_fusion
  140.5 0.2 convolution_select_fusion
  140.7 0.6 reshape.77
  141.3 3.2 %collective-permute-start.7 = (f32[]{:T(128)}, f32[]{:T(128)}, u32[]{:S(2)}, u32[]{:S(2)}) collective-permute-start(f32[]{:T(128)} %get-tuple-element.7), channel_id=1, source_target_pairs={{0,1},{1,0},{2,3},{3,2},{4,5},{5,4},{6,7},{7,6},{8,9},{9,8},{10,11... | collective-permute-start | bytes 20 | tf_op jit(solution)/shard_map/fsd0s1/ppermute | solution.py:66
  144.5 1.0 copy.36
  145.5 1.4 collective-permute-done.7
  148.1 5.5 %collective-permute-start.8 = (f32[]{:T(128)}, f32[]{:T(128)}, u32[]{:S(2)}, u32[]{:S(2)}) collective-permute-start(f32[]{:T(128)} %add.96), channel_id=1, source_target_pairs={{0,2},{1,3},{2,0},{3,1},{4,6},{5,7},{6,4},{7,5},{8,10},{9,11},{10,... | collective-permute-start | bytes 20 | tf_op jit(solution)/shard_map/fsd1s1/ppermute | solution.py:66
  153.6 0.8 collective-permute-done.8
  155.1 8.7 %collective-permute-start.9 = (f32[]{:T(128)}, f32[]{:T(128)}, u32[]{:S(2)}, u32[]{:S(2)}) collective-permute-start(f32[]{:T(128)} %add.97), channel_id=1, source_target_pairs={{0,4},{1,5},{2,6},{3,7},{4,0},{5,1},{6,2},{7,3},{8,12},{9,13},{10,... | collective-permute-start | bytes 20 | tf_op jit(solution)/shard_map/fsd2s1/ppermute | solution.py:66
  163.8 0.6 collective-permute-done.9
  165.1 35.3 %shard_map.95 = bf16[1024,512]{1,0:T(8,128)(2,1)} custom-call(f32[64,64]{1,0:T(8,128)} %cosine_multiply_fusion.cos_ref, s32[16,64,8]{2,1,0:T(8,128)} %bitcast.15, f32[16,64,8]{2,1,0:T(8,128)} %bitcast.16, f32[1,1]{1,0:T(1,128)} %bitcast.10.scale_ref, bf16[1024,512]{1,0:T(8,128)(2,1)} %p_ref.1), custom_call_target="tpu_custom_call" | custom-call | tf_op jit(solution)/shard_map/pallas_call | solution.py:161
  (13 shorter events, 0.2 us)
Async XLA Ops:
  0.6 4.2 %copy-start = (s32[128,64]{0,1:T(8,128)S(1)}, s32[128,64]{0,1:T(8,128)}, u32[]{:S(2)}) copy-start(s32[128,64]{0,1:T(8,128)} %param.12) | copy-start | bytes 98308
  4.0 0.7 copy-start.1
  73.3 3.2 %collective-permute-start = (f32[258,64]{1,0:T(8,128)S(1)}, f32[258,64]{1,0:T(8,128)S(1)}, u32[]{:S(2)}, u32[]{:S(2)}) collective-permute-start(f32[258,64]{1,0:T(8,128)S(1)} %pad_maximum_fusion), channel_id=1, source_target_pairs={{0,8},{8,0},{16,24},{24,16},{32,40},{40,32},{48,56},{56,48},{64,72... | collective-permute-start | bytes 198152 | tf_op jit(solution)/shard_map/isl0s1/ppermute | solution.py:66
  76.6 7.5 %collective-permute-start.1 = (f32[258,64]{1,0:T(8,128)S(1)}, f32[258,64]{1,0:T(8,128)S(1)}, u32[]{:S(2)}, u32[]{:S(2)}) collective-permute-start(f32[258,64]{1,0:T(8,128)S(1)} %fusion.14), channel_id=1, source_target_pairs={{0,16},{8,24},{16,0},{24,8},{32,48},{40,56},{48,32},{56,40},{64,80... | collective-permute-start | bytes 198152 | tf_op jit(solution)/shard_map/isl1s1/ppermute | solution.py:66
  84.1 13.8 %collective-permute-start.2 = (f32[258,64]{1,0:T(8,128)S(1)}, f32[258,64]{1,0:T(8,128)S(1)}, u32[]{:S(2)}, u32[]{:S(2)}) collective-permute-start(f32[258,64]{1,0:T(8,128)S(1)} %add.87), channel_id=1, source_target_pairs={{0,32},{8,40},{16,48},{24,56},{32,0},{40,8},{48,16},{56,24},{64,96... | collective-permute-start | bytes 198152 | tf_op jit(solution)/shard_map/isl2s1/ppermute | solution.py:66
  97.9 19.0 %collective-permute-start.4 = (f32[258,64]{1,0:T(8,128)S(1)}, f32[258,64]{1,0:T(8,128)S(1)}, u32[]{:S(2)}, u32[]{:S(2)}) collective-permute-start(f32[258,64]{1,0:T(8,128)S(1)} %add.88), channel_id=1, source_target_pairs={{0,64},{8,72},{16,80},{24,88},{32,96},{40,104},{48,112},{56,120},{... | collective-permute-start | bytes 198152 | tf_op jit(solution)/shard_map/isl3s1/ppermute | solution.py:66
  105.3 18.5 %collective-permute-start.3 = (f32[258,64]{1,0:T(8,128)S(1)}, f32[258,64]{1,0:T(8,128)S(1)}, u32[]{:S(2)}, u32[]{:S(2)}) collective-permute-start(f32[258,64]{1,0:T(8,128)S(1)} %add.88), channel_id=1, source_target_pairs={{0,128},{8,136},{16,144},{24,152},{32,160},{40,168},{48,176},{56,1... | collective-permute-start | bytes 198152 | tf_op jit(solution)/shard_map/isl3s2/ppermute | solution.py:66
  123.8 7.4 %collective-permute-start.5 = (f32[258,64]{1,0:T(8,128)S(1)}, f32[258,64]{1,0:T(8,128)S(1)}, u32[]{:S(2)}, u32[]{:S(2)}) collective-permute-start(f32[258,64]{1,0:T(8,128)S(1)} %select_add_fusion), channel_id=1, source_target_pairs={{0,192},{8,200},{16,208},{24,216},{32,224},{40,232},{48,240},{56,2... | collective-permute-start | bytes 198152 | tf_op jit(solution)/shard_map/isl4s1/ppermute | solution.py:66
  131.3 8.4 %collective-permute-start.6 = (f32[258,64]{1,0:T(8,128)S(1)}, f32[258,64]{1,0:T(8,128)S(1)}, u32[]{:S(2)}, u32[]{:S(2)}) collective-permute-start(f32[258,64]{1,0:T(8,128)S(1)} %add.92), channel_id=1, source_target_pairs={{0,384},{8,392},{16,400},{24,408},{32,416},{40,424},{48,432},{56,4... | collective-permute-start | bytes 198152 | tf_op jit(solution)/shard_map/isl5s1/ppermute | solution.py:66
  141.3 5.5 %collective-permute-start.7 = (f32[]{:T(128)}, f32[]{:T(128)}, u32[]{:S(2)}, u32[]{:S(2)}) collective-permute-start(f32[]{:T(128)} %get-tuple-element.7), channel_id=1, source_target_pairs={{0,1},{1,0},{2,3},{3,2},{4,5},{5,4},{6,7},{7,6},{8,9},{9,8},{10,11... | collective-permute-start | bytes 20 | tf_op jit(solution)/shard_map/fsd0s1/ppermute | solution.py:66
  148.1 6.3 %collective-permute-start.8 = (f32[]{:T(128)}, f32[]{:T(128)}, u32[]{:S(2)}, u32[]{:S(2)}) collective-permute-start(f32[]{:T(128)} %add.96), channel_id=1, source_target_pairs={{0,2},{1,3},{2,0},{3,1},{4,6},{5,7},{6,4},{7,5},{8,10},{9,11},{10,... | collective-permute-start | bytes 20 | tf_op jit(solution)/shard_map/fsd1s1/ppermute | solution.py:66
  155.1 9.3 %collective-permute-start.9 = (f32[]{:T(128)}, f32[]{:T(128)}, u32[]{:S(2)}, u32[]{:S(2)}) collective-permute-start(f32[]{:T(128)} %add.97), channel_id=1, source_target_pairs={{0,4},{1,5},{2,6},{3,7},{4,0},{5,1},{6,2},{7,3},{8,12},{9,13},{10,... | collective-permute-start | bytes 20 | tf_op jit(solution)/shard_map/fsd2s1/ppermute | solution.py:66

commit v4 on v3

--- a/solution.py
+++ b/solution.py
@@ -94,84 +94,88 @@
     return out
 
 
-def _rows(idx_col, cos):
-    hot = (idx_col == lax.broadcasted_iota(jnp.int32, (idx_col.shape[0], 64), 1)).astype(jnp.float32)
-    return jnp.dot(hot, cos, precision=precise_mode, preferred_element_type=jnp.float32)
-
-
-def _encode_kernel(cos_ref, idx_ref, mask_ref, g_ref, e_ref, sent_ref, err_ref):
-    cos = cos_ref[...]
-    for cb in range(idx_ref.shape[2]):
-        cols = slice(cb * 64, (cb + 1) * 64)
-        idx = idx_ref[0, :, cb : cb + 1]
-        row_cos = _rows(idx // 64, cos)
-        col_cos = _rows(idx % 64, cos)
-        x = g_ref[:, cols].astype(jnp.float32) + e_ref[:, cols].astype(jnp.float32)
-        half = jnp.dot(row_cos, x, precision=precise_mode, preferred_element_type=jnp.float32)
-        sent = jnp.sum(half * col_cos, axis=1, keepdims=True) * mask_ref[0, :, cb : cb + 1]
-        sent_ref[0, :, cb : cb + 1] = sent
-        rebuilt = jnp.dot((row_cos * sent).T, col_cos, precision=precise_mode, preferred_element_type=jnp.float32)
-        err_ref[:, cols] = (x - rebuilt).astype(err_ref.dtype)
-
-
-def encode(grad, error, idx_t3, mask3):
+def _slab_tables(idx, cos, tile):
+    count = idx.shape[0]
+    lanes = lax.broadcasted_iota(jnp.int32, (count, 64), 1)
+    row_hot = (idx // 64 == lanes).astype(jnp.float32)
+    col_hot = (idx % 64 == lanes).astype(jnp.float32)
+    row_cos = jnp.dot(row_hot, cos, precision=precise_mode, preferred_element_type=jnp.float32)
+    col_cos = jnp.dot(col_hot, cos, precision=precise_mode, preferred_element_type=jnp.float32)
+    spread = jnp.dot(col_cos, tile, precision=precise_mode, preferred_element_type=jnp.float32)
+    width = tile.shape[1]
+    own = (lax.broadcasted_iota(jnp.int32, (count, width), 0) // 64) == (
+        lax.broadcasted_iota(jnp.int32, (count, width), 1) // 64
+    )
+    return row_cos, jnp.where(own, spread, 0.0)
+
+
+def _encode_kernel(cos_ref, tile_ref, idx_ref, mask_ref, g_ref, e_ref, sent_ref, err_ref):
+    row_cos, col_diag = _slab_tables(idx_ref[0], cos_ref[...], tile_ref[...])
+    x = g_ref[...].astype(jnp.float32) + e_ref[...].astype(jnp.float32)
+    half = jnp.dot(row_cos, x, precision=precise_mode, preferred_element_type=jnp.float32)
+    sent = jnp.sum(half * col_diag, axis=1, keepdims=True) * mask_ref[0]
+    sent_ref[0] = sent
+    rebuilt = jnp.dot((row_cos * sent).T, col_diag, precision=precise_mode, preferred_element_type=jnp.float32)
+    err_ref[...] = (x - rebuilt).astype(err_ref.dtype)
+
+
+def _tile_of(columns):
+    return jnp.tile(jnp.eye(64, dtype=jnp.float32), (1, columns // 64))
+
+
+def encode(grad, error, idx_col, mask_col):
     rows, columns = grad.shape
     row_blocks = rows // 64
-    col_blocks = columns // 64
+    count = idx_col.shape[1]
     return pl.pallas_call(
         _encode_kernel,
         grid=(row_blocks,),
         in_specs=[
             pl.BlockSpec((64, 64), lambda i: (0, 0)),
-            pl.BlockSpec((1, 64, col_blocks), lambda i: (i, 0, 0)),
-            pl.BlockSpec((1, 1, col_blocks), lambda i: (i, 0, 0)),
+            pl.BlockSpec((64, columns), lambda i: (0, 0)),
+            pl.BlockSpec((1, count, 1), lambda i: (i, 0, 0)),
+            pl.BlockSpec((1, count, 1), lambda i: (i, 0, 0)),
             pl.BlockSpec((64, columns), lambda i: (i, 0)),
             pl.BlockSpec((64, columns), lambda i: (i, 0)),
         ],
         out_specs=[
-            pl.BlockSpec((1, 64, col_blocks), lambda i: (i, 0, 0)),
+            pl.BlockSpec((1, count, 1), lambda i: (i, 0, 0)),
             pl.BlockSpec((64, columns), lambda i: (i, 0)),
         ],
         out_shape=[
-            jax.ShapeDtypeStruct((row_blocks, 64, col_blocks), jnp.float32),
+            jax.ShapeDtypeStruct((row_blocks, count, 1), jnp.float32),
             jax.ShapeDtypeStruct((rows, columns), jnp.bfloat16),
         ],
         compiler_params=pltpu.CompilerParams(dimension_semantics=("parallel",)),
-    )(cosine_table(), idx_t3, mask3, grad, error)
-
-
-def _apply_kernel(rate, cos_ref, idx_ref, coef_ref, scale_ref, p_ref, out_ref):
-    cos = cos_ref[...]
-    scale = scale_ref[0, 0]
-    for cb in range(idx_ref.shape[2]):
-        cols = slice(cb * 64, (cb + 1) * 64)
-        idx = idx_ref[0, :, cb : cb + 1]
-        row_cos = _rows(idx // 64, cos)
-        col_cos = _rows(idx % 64, cos)
-        coef = coef_ref[0, :, cb : cb + 1]
-        update = jnp.dot((row_cos * coef).T, col_cos, precision=precise_mode, preferred_element_type=jnp.float32)
-        update = update.astype(jnp.bfloat16).astype(jnp.float32)
-        out_ref[:, cols] = (p_ref[:, cols].astype(jnp.float32) - rate * update / scale).astype(out_ref.dtype)
-
-
-def apply_update(params, idx_t3, coef3, scale, rate):
+    )(cosine_table(), _tile_of(columns), idx_col, mask_col, grad, error)
+
+
+def _apply_kernel(rate, cos_ref, tile_ref, idx_ref, coef_ref, scale_ref, p_ref, out_ref):
+    row_cos, col_diag = _slab_tables(idx_ref[0], cos_ref[...], tile_ref[...])
+    update = jnp.dot((row_cos * coef_ref[0]).T, col_diag, precision=precise_mode, preferred_element_type=jnp.float32)
+    update = update.astype(jnp.bfloat16).astype(jnp.float32)
+    out_ref[...] = (p_ref[...].astype(jnp.float32) - rate * update / scale_ref[0, 0]).astype(out_ref.dtype)
+
+
+def apply_update(params, idx_col, coef_col, scale, rate):
     rows, columns = params.shape
     row_blocks = rows // 64
-    col_blocks = columns // 64
+    count = idx_col.shape[1]
     return pl.pallas_call(
         functools.partial(_apply_kernel, rate),
         grid=(row_blocks,),
         in_specs=[
             pl.BlockSpec((64, 64), lambda i: (0, 0)),
-            pl.BlockSpec((1, 64, col_blocks), lambda i: (i, 0, 0)),
-            pl.BlockSpec((1, 64, col_blocks), lambda i: (i, 0, 0)),
+            pl.BlockSpec((64, columns), lambda i: (0, 0)),
+            pl.BlockSpec((1, count, 1), lambda i: (i, 0, 0)),
+            pl.BlockSpec((1, count, 1), lambda i: (i, 0, 0)),
             pl.BlockSpec(memory_space=pltpu.SMEM),
             pl.BlockSpec((64, columns), lambda i: (i, 0)),
         ],
         out_specs=pl.BlockSpec((64, columns), lambda i: (i, 0)),
         out_shape=jax.ShapeDtypeStruct((rows, columns), jnp.bfloat16),
         compiler_params=pltpu.CompilerParams(dimension_semantics=("parallel",)),
-    )(cosine_table(), idx_t3, coef3, scale.reshape(1, 1), params)
+    )(cosine_table(), _tile_of(columns), idx_col, coef_col, scale.reshape(1, 1), params)
 
 
 def on_device(island_radices, fsdp_radices, pseudo_grad, error_buf, params, momentum, sel_blocks, coef_index, owner_map):
@@ -187,10 +191,12 @@
     chosen = sel_blocks[0]
     block_ids = jnp.arange(n_blocks, dtype=jnp.int32)
     chosen_mask = jnp.any(chosen[:, None] == block_ids[None, :], axis=0).astype(jnp.float32)
-    idx_t3 = coef_index.reshape(row_blocks, col_blocks, coef_total).transpose(0, 2, 1)
-    sent3, fresh_error = encode(pseudo_grad[0], error_buf[0], idx_t3, chosen_mask.reshape(row_blocks, 1, col_blocks))
+    slab = col_blocks * coef_total
+    idx_col = coef_index.reshape(row_blocks, slab, 1)
+    mask_col = jnp.repeat(chosen_mask, coef_total).reshape(row_blocks, slab, 1)
+    sent_col, fresh_error = encode(pseudo_grad[0], error_buf[0], idx_col, mask_col)
     new_error = fresh_error[None]
-    outgoing = sent3.transpose(0, 2, 1).reshape(n_blocks, coef_total)
+    outgoing = sent_col.reshape(n_blocks, coef_total)
 
     earlier = (owner_map[None, :] == owner_map[:, None]) & (block_ids[None, :] < block_ids[:, None])
     slot_of = jnp.sum(earlier.astype(jnp.int32), axis=1)
@@ -221,8 +227,8 @@
     total_square = butterfly_sum(local_square, "fsdp", fsdp_radices, "fsd")
     scale_root = jnp.sqrt(total_square / (shard_rows * lax.axis_size("fsdp") * columns) + EPSILON)
 
-    coef3 = update_coef.reshape(row_blocks, col_blocks, coef_total).transpose(0, 2, 1)
-    new_params = apply_update(params, idx_t3, coef3, scale_root, OUTER_RATE)
+    coef_col = update_coef.reshape(row_blocks, slab, 1)
+    new_params = apply_update(params, idx_col, coef_col, scale_root, OUTER_RATE)
     return (new_params, new_error, new_momentum)
 
 

time: 201 us -> 211 us (1.050)
  the two profiles are of different devices: /device:TPU:192 before, /device:TPU:82 now
where the time goes in v4:
time: 211 us; the launch traced here: 210 us
  Pallas kernels  92.8 us (44%)
  starting transfers between devices  43.5 us (21%)
  waiting for transfers between devices  42.5 us (20%)
  local copies, waits for them, and re-layouts  19.1 us (9%)
  other arithmetic  8.78 us (4%)
  between operations  3.27 us (2%)
    pallas_call x1, Pallas kernels, encode(): pl.pallas_call(_encode_kernel, grid=(row_blocks,), in_specs=[pl.BlockSpec...  56 us
    ppermute x10, starting transfers between devices, butterfly_sum(): pieces[shift] = lax.ppermute(value, axis, perm)  43.5 us
    ppermute x10, waiting for transfers between devices, butterfly_sum(): pieces[shift] = lax.ppermute(value, axis, perm)  42.5 us
    pallas_call x1, Pallas kernels, apply_update(): pl.pallas_call(functools.partial(_apply_kernel, rate), grid=(row_blocks,)...  36.8 us
    broadcast_in_dim x2, local copies, waits for them, and re-layouts, on_device(): mask_col = jnp.repeat(chosen_mask, coef_total).reshape(row_blocks, slab, 1)  5.63 us
    reshape x1, local copies, waits for them, and re-layouts, on_device(): coef_col = update_coef.reshape(row_blocks, slab, 1)  5.55 us
    reshape x1, local copies, waits for them, and re-layouts, on_device(): idx_col = coef_index.reshape(row_blocks, slab, 1)  5.5 us
  transfers between devices with their start and end apart: 10, of which 9 were waited for; matrix products, arithmetic and copies ran while one was open for 3% of the time, Pallas kernels for 0%

profile of v4, /device:TPU:82, one launch (start us, length us, event | category | flops | bytes accessed | tf_op | source)
XLA Modules:
  0.0 210.5 jit_solution(12147459884612581803)
XLA Ops:
  0.6 0.0 copy-start
  0.7 0.7 fusion.4
  1.4 0.1 reshape.83
  1.5 0.1 reshape.84
  1.6 0.9 convert_reduce_fusion
  2.5 0.7 multiply_add_fusion.1
  3.2 0.5 broadcast.96
  3.7 1.3 reduce.4
  5.0 0.1 reshape_squeeze.3
  5.1 0.1 broadcast_in_dim.41
  5.2 5.6 %broadcast_in_dim.45.mask_ref = f32[16,512,1]{2,1,0:T(8,128)} reshape(f32[16,8,64]{2,1,0:T(8,128)S(1)} %broadcast_in_dim.41) | data formatting | bytes 65536 | tf_op jit(solution)/shard_map/broadcast_in_dim | solution.py:196
  10.7 0.0 copy-done
  10.7 0.1 copy.33
  10.8 5.5 %reshape.86.idx_ref = s32[16,512,1]{2,1,0:T(8,128)} reshape(s32[128,64]{1,0:T(8,128)S(1)} %copy.33) | data formatting | bytes 65536 | tf_op jit(solution)/shard_map/reshape | solution.py:195
  16.3 0.8 tile.9.tile_ref
  17.1 0.7 cosine_multiply_fusion.cos_ref
  17.8 56.0 %shard_map.94 = (f32[16,512,1]{2,1,0:T(8,128)}, bf16[1024,512]{1,0:T(8,128)(2,1)}) custom-call(f32[64,64]{1,0:T(8,128)} %cosine_multiply_fusion.cos_ref, f32[64,512]{1,0:T(8,128)} %tile.9.tile_ref, s32[16,512,1]{2,1,0:T(8,128)} %reshape.86.idx_ref, f32[16,512,1]{2,1,0:T(8,128)} %broadcast_in_dim.45.mask_ref, bf16[1024,512]{1,0:T(8,128)(2,1)} %bitcast.6, ...), custom_call_target="tpu_custom_call" | custom-call | tf_op jit(solution)/shard_map/pallas_call | solution.py:130
  73.8 3.3 %reduce = f32[16,512]{1,0:T(8,128)S(1)} reduce(f32[16,512,1]{2,1,0:T(8,128)} %get-tuple-element.5, f32[]{:T(128)} %constant.81), dimensions={2}, to_apply=%get-tuple-element.5.reduce_sub_computation | reduce | bytes 65540 | tf_op jit(solution)/shard_map/pallas_call | solution.py:130
  77.2 0.1 reshape.79
  77.2 0.3 fusion.6
  77.6 1.9 collective-permute-start
  79.5 1.3 collective-permute-done
  80.9 1.9 collective-permute-start.1
  82.8 5.6 %collective-permute-done.1 = f32[258,64]{1,0:T(8,128)S(1)} collective-permute-done((f32[258,64]{1,0:T(8,128)S(1)}, f32[258,64]{1,0:T(8,128)S(1)}, u32[]{:S(2)}, u32[]{:S(2)}) %collective-permute-start.1) | collective-permute-done | bytes 66080 | tf_op jit(solution)/shard_map/isl1s1/ppermute | solution.py:66
  88.4 6.1 %collective-permute-start.2 = (f32[258,64]{1,0:T(8,128)S(1)}, f32[258,64]{1,0:T(8,128)S(1)}, u32[]{:S(2)}, u32[]{:S(2)}) collective-permute-start(f32[258,64]{1,0:T(8,128)S(1)} %add.87), channel_id=1, source_target_pairs={{0,32},{8,40},{16,48},{24,56},{32,0},{40,8},{48,16},{56,24},{64,96... | collective-permute-start | bytes 198152 | tf_op jit(solution)/shard_map/isl2s1/ppermute | solution.py:66
  94.5 5.2 %collective-permute-done.2 = f32[258,64]{1,0:T(8,128)S(1)} collective-permute-done((f32[258,64]{1,0:T(8,128)S(1)}, f32[258,64]{1,0:T(8,128)S(1)}, u32[]{:S(2)}, u32[]{:S(2)}) %collective-permute-start.2) | collective-permute-done | bytes 66080 | tf_op jit(solution)/shard_map/isl2s1/ppermute | solution.py:66
  99.7 11.8 %collective-permute-start.3 = (f32[258,64]{1,0:T(8,128)S(1)}, f32[258,64]{1,0:T(8,128)S(1)}, u32[]{:S(2)}, u32[]{:S(2)}) collective-permute-start(f32[258,64]{1,0:T(8,128)S(1)} %add.88), channel_id=1, source_target_pairs={{0,128},{8,136},{16,144},{24,152},{32,160},{40,168},{48,176},{56,1... | collective-permute-start | bytes 198152 | tf_op jit(solution)/shard_map/isl3s2/ppermute | solution.py:66
  111.6 1.9 collective-permute-start.4
  113.6 2.2 %collective-permute-done.3 = f32[258,64]{1,0:T(8,128)S(1)} collective-permute-done((f32[258,64]{1,0:T(8,128)S(1)}, f32[258,64]{1,0:T(8,128)S(1)}, u32[]{:S(2)}, u32[]{:S(2)}) %collective-permute-start.3) | collective-permute-done | bytes 66080 | tf_op jit(solution)/shard_map/isl3s2/ppermute | solution.py:66
  115.7 13.5 %collective-permute-done.4 = f32[258,64]{1,0:T(8,128)S(1)} collective-permute-done((f32[258,64]{1,0:T(8,128)S(1)}, f32[258,64]{1,0:T(8,128)S(1)}, u32[]{:S(2)}, u32[]{:S(2)}) %collective-permute-start.4) | collective-permute-done | bytes 66080 | tf_op jit(solution)/shard_map/isl3s1/ppermute | solution.py:66
  129.3 2.4 %collective-permute-start.5 = (f32[258,64]{1,0:T(8,128)S(1)}, f32[258,64]{1,0:T(8,128)S(1)}, u32[]{:S(2)}, u32[]{:S(2)}) collective-permute-start(f32[258,64]{1,0:T(8,128)S(1)} %select_add_fusion), channel_id=1, source_target_pairs={{0,192},{8,200},{16,208},{24,216},{32,224},{40,232},{48,240},{56,2... | collective-permute-start | bytes 198152 | tf_op jit(solution)/shard_map/isl4s1/ppermute | solution.py:66
  131.7 0.2 fusion.8
  131.9 4.3 %collective-permute-done.5 = f32[258,64]{1,0:T(8,128)S(1)} collective-permute-done((f32[258,64]{1,0:T(8,128)S(1)}, f32[258,64]{1,0:T(8,128)S(1)}, u32[]{:S(2)}, u32[]{:S(2)}) %collective-permute-start.5) | collective-permute-done | bytes 66080 | tf_op jit(solution)/shard_map/isl4s1/ppermute | solution.py:66
  136.2 4.0 %collective-permute-start.6 = (f32[258,64]{1,0:T(8,128)S(1)}, f32[258,64]{1,0:T(8,128)S(1)}, u32[]{:S(2)}, u32[]{:S(2)}) collective-permute-start(f32[258,64]{1,0:T(8,128)S(1)} %add.92), channel_id=1, source_target_pairs={{0,384},{8,392},{16,400},{24,408},{32,416},{40,424},{48,432},{56,4... | collective-permute-start | bytes 198152 | tf_op jit(solution)/shard_map/isl5s1/ppermute | solution.py:66
  140.2 4.4 %collective-permute-done.6 = f32[258,64]{1,0:T(8,128)S(1)} collective-permute-done((f32[258,64]{1,0:T(8,128)S(1)}, f32[258,64]{1,0:T(8,128)S(1)}, u32[]{:S(2)}, u32[]{:S(2)}) %collective-permute-start.6) | collective-permute-done | bytes 66080 | tf_op jit(solution)/shard_map/isl5s1/ppermute | solution.py:66
  144.6 0.1 max.15
  144.7 0.7 multiply_reduce_fusion
  145.4 0.2 convolution_select_fusion
  145.6 0.6 reshape.82
  146.3 3.5 %collective-permute-start.7 = (f32[]{:T(128)}, f32[]{:T(128)}, u32[]{:S(2)}, u32[]{:S(2)}) collective-permute-start(f32[]{:T(128)} %get-tuple-element.7), channel_id=1, source_target_pairs={{0,1},{1,0},{2,3},{3,2},{4,5},{5,4},{6,7},{7,6},{8,9},{9,8},{10,11... | collective-permute-start | bytes 20 | tf_op jit(solution)/shard_map/fsd0s1/ppermute | solution.py:66
  149.7 5.6 %reshape.85.coef_ref = f32[16,512,1]{2,1,0:T(8,128)} reshape(f32[128,64]{1,0:T(8,128)S(1)} %get-tuple-element.8) | data formatting | bytes 65536 | tf_op jit(solution)/shard_map/reshape | solution.py:230
  155.3 0.0 collective-permute-done.7
  156.5 3.5 %collective-permute-start.8 = (f32[]{:T(128)}, f32[]{:T(128)}, u32[]{:S(2)}, u32[]{:S(2)}) collective-permute-start(f32[]{:T(128)} %add.96), channel_id=1, source_target_pairs={{0,2},{1,3},{2,0},{3,1},{4,6},{5,7},{6,4},{7,5},{8,10},{9,11},{10,... | collective-permute-start | bytes 20 | tf_op jit(solution)/shard_map/fsd1s1/ppermute | solution.py:66
  160.0 2.9 %collective-permute-done.8 = f32[]{:T(128)} collective-permute-done((f32[]{:T(128)}, f32[]{:T(128)}, u32[]{:S(2)}, u32[]{:S(2)}) %collective-permute-start.8) | collective-permute-done | bytes 36 | tf_op jit(solution)/shard_map/fsd1s1/ppermute | solution.py:66
  163.6 6.3 %collective-permute-start.9 = (f32[]{:T(128)}, f32[]{:T(128)}, u32[]{:S(2)}, u32[]{:S(2)}) collective-permute-start(f32[]{:T(128)} %add.97), channel_id=1, source_target_pairs={{0,4},{1,5},{2,6},{3,7},{4,0},{5,1},{6,2},{7,3},{8,12},{9,13},{10,... | collective-permute-start | bytes 20 | tf_op jit(solution)/shard_map/fsd2s1/ppermute | solution.py:66
  169.9 3.2 %collective-permute-done.9 = f32[]{:T(128)} collective-permute-done((f32[]{:T(128)}, f32[]{:T(128)}, u32[]{:S(2)}, u32[]{:S(2)}) %collective-permute-start.9) | collective-permute-done | bytes 36 | tf_op jit(solution)/shard_map/fsd2s1/ppermute | solution.py:66
  173.6 36.8 %shard_map.95 = bf16[1024,512]{1,0:T(8,128)(2,1)} custom-call(f32[64,64]{1,0:T(8,128)} %cosine_multiply_fusion.cos_ref, f32[64,512]{1,0:T(8,128)} %tile.9.tile_ref, s32[16,512,1]{2,1,0:T(8,128)} %reshape.86.idx_ref, f32[16,512,1]{2,1,0:T(8,128)} %reshape.85.coef_ref, f32[1,1]{1,0:T(1,128)} %bitcast.3.scale_ref, bf16[1024,512]{1,0:T(8,128)(2,1)} %p_ref.1), custom_call_target="tpu_custom_call" | custom-call | tf_op jit(solution)/shard_map/pallas_call | solution.py:164
  (14 shorter events, 0.2 us)
Async XLA Ops:
  0.6 10.1 %copy-start = (s32[128,64]{0,1:T(8,128)S(1)}, s32[128,64]{0,1:T(8,128)}, u32[]{:S(2)}) copy-start(s32[128,64]{0,1:T(8,128)} %param.12) | copy-start | bytes 98308
  77.6 3.2 %collective-permute-start = (f32[258,64]{1,0:T(8,128)S(1)}, f32[258,64]{1,0:T(8,128)S(1)}, u32[]{:S(2)}, u32[]{:S(2)}) collective-permute-start(f32[258,64]{1,0:T(8,128)S(1)} %pad_maximum_fusion), channel_id=1, source_target_pairs={{0,8},{8,0},{16,24},{24,16},{32,40},{40,32},{48,56},{56,48},{64,72... | collective-permute-start | bytes 198152 | tf_op jit(solution)/shard_map/isl0s1/ppermute | solution.py:66
  80.9 7.5 %collective-permute-start.1 = (f32[258,64]{1,0:T(8,128)S(1)}, f32[258,64]{1,0:T(8,128)S(1)}, u32[]{:S(2)}, u32[]{:S(2)}) collective-permute-start(f32[258,64]{1,0:T(8,128)S(1)} %fusion.14), channel_id=1, source_target_pairs={{0,16},{8,24},{16,0},{24,8},{32,48},{40,56},{48,32},{56,40},{64,80... | collective-permute-start | bytes 198152 | tf_op jit(solution)/shard_map/isl1s1/ppermute | solution.py:66
  88.4 11.3 %collective-permute-start.2 = (f32[258,64]{1,0:T(8,128)S(1)}, f32[258,64]{1,0:T(8,128)S(1)}, u32[]{:S(2)}, u32[]{:S(2)}) collective-permute-start(f32[258,64]{1,0:T(8,128)S(1)} %add.87), channel_id=1, source_target_pairs={{0,32},{8,40},{16,48},{24,56},{32,0},{40,8},{48,16},{56,24},{64,96... | collective-permute-start | bytes 198152 | tf_op jit(solution)/shard_map/isl2s1/ppermute | solution.py:66
  99.7 16.0 %collective-permute-start.3 = (f32[258,64]{1,0:T(8,128)S(1)}, f32[258,64]{1,0:T(8,128)S(1)}, u32[]{:S(2)}, u32[]{:S(2)}) collective-permute-start(f32[258,64]{1,0:T(8,128)S(1)} %add.88), channel_id=1, source_target_pairs={{0,128},{8,136},{16,144},{24,152},{32,160},{40,168},{48,176},{56,1... | collective-permute-start | bytes 198152 | tf_op jit(solution)/shard_map/isl3s2/ppermute | solution.py:66
  111.6 17.7 %collective-permute-start.4 = (f32[258,64]{1,0:T(8,128)S(1)}, f32[258,64]{1,0:T(8,128)S(1)}, u32[]{:S(2)}, u32[]{:S(2)}) collective-permute-start(f32[258,64]{1,0:T(8,128)S(1)} %add.88), channel_id=1, source_target_pairs={{0,64},{8,72},{16,80},{24,88},{32,96},{40,104},{48,112},{56,120},{... | collective-permute-start | bytes 198152 | tf_op jit(solution)/shard_map/isl3s1/ppermute | solution.py:66
  129.3 6.9 %collective-permute-start.5 = (f32[258,64]{1,0:T(8,128)S(1)}, f32[258,64]{1,0:T(8,128)S(1)}, u32[]{:S(2)}, u32[]{:S(2)}) collective-permute-start(f32[258,64]{1,0:T(8,128)S(1)} %select_add_fusion), channel_id=1, source_target_pairs={{0,192},{8,200},{16,208},{24,216},{32,224},{40,232},{48,240},{56,2... | collective-permute-start | bytes 198152 | tf_op jit(solution)/shard_map/isl4s1/ppermute | solution.py:66
  136.2 8.4 %collective-permute-start.6 = (f32[258,64]{1,0:T(8,128)S(1)}, f32[258,64]{1,0:T(8,128)S(1)}, u32[]{:S(2)}, u32[]{:S(2)}) collective-permute-start(f32[258,64]{1,0:T(8,128)S(1)} %add.92), channel_id=1, source_target_pairs={{0,384},{8,392},{16,400},{24,408},{32,416},{40,424},{48,432},{56,4... | collective-permute-start | bytes 198152 | tf_op jit(solution)/shard_map/isl5s1/ppermute | solution.py:66
  146.3 9.0 %collective-permute-start.7 = (f32[]{:T(128)}, f32[]{:T(128)}, u32[]{:S(2)}, u32[]{:S(2)}) collective-permute-start(f32[]{:T(128)} %get-tuple-element.7), channel_id=1, source_target_pairs={{0,1},{1,0},{2,3},{3,2},{4,5},{5,4},{6,7},{7,6},{8,9},{9,8},{10,11... | collective-permute-start | bytes 20 | tf_op jit(solution)/shard_map/fsd0s1/ppermute | solution.py:66
  156.5 6.5 %collective-permute-start.8 = (f32[]{:T(128)}, f32[]{:T(128)}, u32[]{:S(2)}, u32[]{:S(2)}) collective-permute-start(f32[]{:T(128)} %add.96), channel_id=1, source_target_pairs={{0,2},{1,3},{2,0},{3,1},{4,6},{5,7},{6,4},{7,5},{8,10},{9,11},{10,... | collective-permute-start | bytes 20 | tf_op jit(solution)/shard_map/fsd1s1/ppermute | solution.py:66
  163.6 9.5 %collective-permute-start.9 = (f32[]{:T(128)}, f32[]{:T(128)}, u32[]{:S(2)}, u32[]{:S(2)}) collective-permute-start(f32[]{:T(128)} %add.97), channel_id=1, source_target_pairs={{0,4},{1,5},{2,6},{3,7},{4,0},{5,1},{6,2},{7,3},{8,12},{9,13},{10,... | collective-permute-start | bytes 20 | tf_op jit(solution)/shard_map/fsd2s1/ppermute | solution.py:66

commit v5 on v1

--- a/solution.py
+++ b/solution.py
@@ -160,10 +160,12 @@
         P("fsdp"),
     )
     out_specs = (P("fsdp", None), P("island", "fsdp", None), P("island", "fsdp"))
-    island_radices = radices_of((4, 12, 2))
-    if mesh.shape["island"] != 96:
-        island_radices = radices_of((mesh.shape["island"],))
+    island_radices = radices_of((mesh.shape["island"],))
+    if mesh.shape["island"] == 96:
+        island_radices = [2, 4, 3, 4]
     fsdp_radices = radices_of((mesh.shape["fsdp"],))
+    if mesh.shape["fsdp"] == 8:
+        fsdp_radices = [2, 4]
     body = functools.partial(on_device, island_radices, fsdp_radices)
     return jax.shard_map(
         body, mesh=mesh, in_specs=in_specs, out_specs=out_specs, check_vma=False

time: 193 us -> 205 us (1.062)
  the two profiles are of different devices: /device:TPU:192 before, /device:TPU:2 now
where the time goes in v5:
time: 205 us; the launch traced here: 201 us
  starting transfers between devices  62.5 us (30%)
  local copies, waits for them, and re-layouts  47.5 us (23%)
  matrix products  38.3 us (19%)
  waiting for transfers between devices  29.9 us (15%)
  other arithmetic  12.5 us (6%)
  between operations  10.3 us (5%)
    ppermute x13, starting transfers between devices, butterfly_sum(): pieces[shift] = lax.ppermute(value, axis, perm)  62.5 us
    ppermute x13, waiting for transfers between devices, butterfly_sum(): pieces[shift] = lax.ppermute(value, axis, perm)  29.9 us
    dot_general x2, matrix products, decode(): jnp.einsum('bkj,bkl->bjl', row_cos * values[:, :, None], col_cos, precisi...  22.4 us
    dot_general x1, matrix products, on_device(): half = jnp.einsum('bkj,bjl->bkl', row_cos, blocks, precision=precise_mode)  11.6 us
    dot_general x2, local copies, waits for them, and re-layouts, one_hot_rows(): return jnp.einsum('...t,tc->...c', hot, table, precision=precise_mode)  10.4 us
    mul x2, local copies, waits for them, and re-layouts, decode(): row_cos * values[:, :, None]  10.3 us
    add x2, local copies, waits for them, and re-layouts, on_device(): pseudo_grad[0].astype(jnp.float32) + error_buf[0].astype(jnp.float32)  9.27 us
    div x2, local copies, waits for them, and re-layouts, on_device(): OUTER_RATE * shifted / scale_root  8.72 us
  transfers between devices with their start and end apart: 13, of which 8 were waited for; matrix products, arithmetic and copies ran while one was open for 0% of the time, Pallas kernels for 0%

profile of v5, /device:TPU:2, one launch (start us, length us, event | category | flops | bytes accessed | tf_op | source)
XLA Modules:
  0.0 201.0 jit_solution(13886336351933738136)
XLA Ops:
  0.7 0.5 broadcast.124
  1.2 1.3 reduce.3
  2.6 0.7 fusion.12
  3.3 0.9 convert_reduce_fusion
  4.2 0.7 multiply_add_fusion.1
  5.0 0.8 add_select_fusion
  5.8 2.6 %fusion.3 = f32[128,64,64]{0,2,1:T(8,128)} fusion(s32[128,64]{0,1:T(8,128)S(1)} %get-tuple-element.5, f32[64]{0:T(128)S(1)} %get-tuple-element.10, f32[64]{0:T(128)S(1)} %get-tuple-element.9), kind=kOutput, calls=%fused_computation.11 | convolution fusion | flops 403189760 | bytes 2130432 | tf_op jit(solution)/shard_map/...t,tc->...c/dot_general | solution.py:43
  8.3 1.2 fusion.2
  9.6 5.9 %copy.51 = f32[128,64,64]{1,2,0:T(8,128)} copy(f32[128,64,64]{0,2,1:T(8,128)} %fusion.3) | data formatting | bytes 4194304 | tf_op jit(solution)/shard_map/...t,tc->...c/dot_general | solution.py:43
  15.5 2.8 %convert_add_fusion = f32[1,1024,512]{2,1,0:T(8,128)} fusion(bf16[1,1024,512]{2,1,0:T(8,128)(2,1)S(1)} %copy-done.1, bf16[1,1024,512]{2,1,0:T(8,128)(2,1)} %param.7), kind=kLoop, calls=%fused_computation.8 | loop fusion | flops 1572864 | bytes 4194304 | tf_op jit(solution)/shard_map/add | solution.py:101
  18.3 4.4 %add.189 = f32[16,64,8,64]{3,2,1,0:T(8,128)} reshape(f32[1,1024,512]{2,1,0:T(8,128)} %convert_add_fusion) | data formatting | bytes 4194304 | tf_op jit(solution)/shard_map/add | solution.py:101
  22.7 4.9 %copy.48 = f32[16,64,8,64]{3,1,2,0:T(8,128)} copy(f32[16,64,8,64]{3,2,1,0:T(8,128)} %add.189) | data formatting | bytes 4194304 | tf_op jit(solution)/shard_map/add | solution.py:101
  27.6 4.5 %copy.49 = f32[128,64,64]{2,1,0:T(8,128)} copy(f32[128,64,64]{0,2,1:T(8,128)S(1)} %fusion.2) | data formatting | bytes 4194304 | tf_op jit(solution)/shard_map/...t,tc->...c/dot_general | solution.py:43
  32.1 11.6 %multiply_reduce_fusion = f32[128,64]{1,0:T(8,128)S(1)} fusion(f32[128,64,64]{1,2,0:T(8,128)} %copy.51, f32[128,64,64]{2,1,0:T(8,128)} %copy.49, f32[128,64,64]{2,1,0:T(8,128)} %bitcast.26), kind=kOutput, calls=%fused_computation.5 | convolution fusion | flops 403693568 | bytes 6324224 | tf_op jit(solution)/shard_map/bkj,bjl->bkl/dot_general | solution.py:105
  43.9 0.3 fusion.21
  44.2 1.9 collective-permute-start
  46.2 1.3 collective-permute-done
  47.5 4.3 %collective-permute-start.3 = (f32[258,64]{1,0:T(8,128)S(1)}, f32[258,64]{1,0:T(8,128)S(1)}, u32[]{:S(2)}, u32[]{:S(2)}) collective-permute-start(f32[258,64]{1,0:T(8,128)S(1)} %fusion.31), channel_id=1, source_target_pairs={{0,16},{8,24},{16,32},{24,40},{32,48},{40,56},{48,0},{56,8},{64,80... | collective-permute-start | bytes 198152 | tf_op jit(solution)/shard_map/ppermute | solution.py:62
  51.8 6.1 %collective-permute-start.2 = (f32[258,64]{1,0:T(8,128)S(1)}, f32[258,64]{1,0:T(8,128)S(1)}, u32[]{:S(2)}, u32[]{:S(2)}) collective-permute-start(f32[258,64]{1,0:T(8,128)S(1)} %fusion.31), channel_id=1, source_target_pairs={{0,32},{8,40},{16,48},{24,56},{32,0},{40,8},{48,16},{56,24},{64,96... | collective-permute-start | bytes 198152 | tf_op jit(solution)/shard_map/ppermute | solution.py:62
  57.9 2.5 %collective-permute-start.1 = (f32[258,64]{1,0:T(8,128)S(1)}, f32[258,64]{1,0:T(8,128)S(1)}, u32[]{:S(2)}, u32[]{:S(2)}) collective-permute-start(f32[258,64]{1,0:T(8,128)S(1)} %fusion.31), channel_id=1, source_target_pairs={{0,48},{8,56},{16,0},{24,8},{32,16},{40,24},{48,32},{56,40},{64,11... | collective-permute-start | bytes 198152 | tf_op jit(solution)/shard_map/ppermute | solution.py:62
  60.5 4.7 %collective-permute-done.2 = f32[258,64]{1,0:T(8,128)S(1)} collective-permute-done((f32[258,64]{1,0:T(8,128)S(1)}, f32[258,64]{1,0:T(8,128)S(1)}, u32[]{:S(2)}, u32[]{:S(2)}) %collective-permute-start.2) | collective-permute-done | bytes 66080 | tf_op jit(solution)/shard_map/ppermute | solution.py:62
  65.2 2.4 %collective-permute-done.1 = f32[258,64]{1,0:T(8,128)S(1)} collective-permute-done((f32[258,64]{1,0:T(8,128)S(1)}, f32[258,64]{1,0:T(8,128)S(1)}, u32[]{:S(2)}, u32[]{:S(2)}) %collective-permute-start.1) | collective-permute-done | bytes 66080 | tf_op jit(solution)/shard_map/ppermute | solution.py:62
  67.6 10.6 %collective-permute-start.5 = (f32[258,64]{1,0:T(8,128)S(1)}, f32[258,64]{1,0:T(8,128)S(1)}, u32[]{:S(2)}, u32[]{:S(2)}) collective-permute-start(f32[258,64]{1,0:T(8,128)S(1)} %select_add_fusion.2), channel_id=1, source_target_pairs={{0,64},{8,72},{16,80},{24,88},{32,96},{40,104},{48,112},{56,120},{... | collective-permute-start | bytes 198152 | tf_op jit(solution)/shard_map/ppermute | solution.py:62
  78.3 3.1 %collective-permute-start.4 = (f32[258,64]{1,0:T(8,128)S(1)}, f32[258,64]{1,0:T(8,128)S(1)}, u32[]{:S(2)}, u32[]{:S(2)}) collective-permute-start(f32[258,64]{1,0:T(8,128)S(1)} %select_add_fusion.2), channel_id=1, source_target_pairs={{0,128},{8,136},{16,144},{24,152},{32,160},{40,168},{48,176},{56,1... | collective-permute-start | bytes 198152 | tf_op jit(solution)/shard_map/ppermute | solution.py:62
  81.6 1.3 collective-permute-done.5
  82.9 14.5 %collective-permute-done.4 = f32[258,64]{1,0:T(8,128)S(1)} collective-permute-done((f32[258,64]{1,0:T(8,128)S(1)}, f32[258,64]{1,0:T(8,128)S(1)}, u32[]{:S(2)}, u32[]{:S(2)}) %collective-permute-start.4) | collective-permute-done | bytes 66080 | tf_op jit(solution)/shard_map/ppermute | solution.py:62
  97.5 3.4 %collective-permute-start.8 = (f32[258,64]{1,0:T(8,128)S(1)}, f32[258,64]{1,0:T(8,128)S(1)}, u32[]{:S(2)}, u32[]{:S(2)}) collective-permute-start(f32[258,64]{1,0:T(8,128)S(1)} %select_add_fusion.1), channel_id=1, source_target_pairs={{0,192},{8,200},{16,208},{24,216},{32,224},{40,232},{48,240},{56,2... | collective-permute-start | bytes 198152 | tf_op jit(solution)/shard_map/ppermute | solution.py:62
  100.9 3.0 %collective-permute-start.7 = (f32[258,64]{1,0:T(8,128)S(1)}, f32[258,64]{1,0:T(8,128)S(1)}, u32[]{:S(2)}, u32[]{:S(2)}) collective-permute-start(f32[258,64]{1,0:T(8,128)S(1)} %select_add_fusion.1), channel_id=1, source_target_pairs={{0,384},{8,392},{16,400},{24,408},{32,416},{40,424},{48,432},{56,4... | collective-permute-start | bytes 198152 | tf_op jit(solution)/shard_map/ppermute | solution.py:62
  103.9 4.6 %collective-permute-start.6 = (f32[258,64]{1,0:T(8,128)S(1)}, f32[258,64]{1,0:T(8,128)S(1)}, u32[]{:S(2)}, u32[]{:S(2)}) collective-permute-start(f32[258,64]{1,0:T(8,128)S(1)} %select_add_fusion.1), channel_id=1, source_target_pairs={{0,576},{8,584},{16,592},{24,600},{32,608},{40,616},{48,624},{56,6... | collective-permute-start | bytes 198152 | tf_op jit(solution)/shard_map/ppermute | solution.py:62
  108.8 1.7 collective-permute-done.7
  110.5 1.9 collective-permute-done.6
  113.0 0.6 reshape.105
  113.6 2.7 %broadcast_multiply_fusion = (f32[128,64,64]{0,2,1:T(8,128)}, f32[128,64,64]{0,2,1:T(8,128)}) fusion(f32[128,64,64]{0,2,1:T(8,128)S(1)} %fusion.2, f32[128,64]{0,1:T(8,128)S(1)} %copy.57, f32[128,64]{0,1:T(8,128)S(1)} %copy.53), kind=kLoop, calls=%fused_computation.14 | loop fusion | flops 1048576 | bytes 6356992 | tf_op jit(solution)/shard_map/mul | solution.py:47
  116.3 5.7 %copy.58 = f32[128,64,64]{1,2,0:T(8,128)} copy(f32[128,64,64]{0,2,1:T(8,128)} %get-tuple-element.3) | data formatting | bytes 4194304 | tf_op jit(solution)/shard_map/mul | solution.py:47
  122.0 11.5 %subtract_convert_fusion = bf16[128,64,64]{2,1,0:T(8,128)(2,1)S(1)} fusion(f32[128,64,64]{2,1,0:T(8,128)} %bitcast.27, f32[128,64,64]{1,2,0:T(8,128)} %copy.58, f32[128,64,64]{1,2,0:T(8,128)} %copy.51), kind=kOutput, calls=%fused_computation.4 | convolution fusion | flops 403701760 | bytes 7340032 | tf_op jit(solution)/shard_map/bkj,bkl->bjl/dot_general | solution.py:47
  133.5 3.1 %copy.60 = bf16[16,64,8,64]{3,2,1,0:T(8,128)(2,1)} copy(bf16[16,64,8,64]{3,1,2,0:T(8,128)(2,1)S(1)} %bitcast.29) | data formatting | bytes 2097152 | tf_op jit(solution)/shard_map/convert_element_type | solution.py:130
  136.6 4.0 %convert_element_type.75 = bf16[1,1024,512]{2,1,0:T(8,128)(2,1)} reshape(bf16[16,64,8,64]{3,2,1,0:T(8,128)(2,1)} %copy.60) | data formatting | bytes 2097152 | tf_op jit(solution)/shard_map/convert_element_type | solution.py:130
  140.7 4.7 %copy.54 = f32[128,64,64]{1,2,0:T(8,128)} copy(f32[128,64,64]{0,2,1:T(8,128)S(1)} %copy-done) | data formatting | bytes 4194304 | tf_op jit(solution)/shard_map/mul | solution.py:47
  145.4 10.9 %fusion.1 = (f32[]{:T(128)}, bf16[128,64,64]{2,1,0:T(8,128)(2,1)S(1)}) fusion(f32[128,64,64]{1,2,0:T(8,128)} %copy.54, f32[128,64,64]{1,2,0:T(8,128)} %copy.51), kind=kOutput, calls=%fused_computation.3 | convolution fusion | flops 404750336 | bytes 5242884 | tf_op jit(solution)/shard_map/bkj,bkl->bjl/dot_general | solution.py:47
  156.3 3.5 %collective-permute-start.9 = (f32[]{:T(128)}, f32[]{:T(128)}, u32[]{:S(2)}, u32[]{:S(2)}) collective-permute-start(f32[]{:T(128)} %get-tuple-element.7), channel_id=1, source_target_pairs={{0,1},{1,0},{2,3},{3,2},{4,5},{5,4},{6,7},{7,6},{8,9},{9,8},{10,11... | collective-permute-start | bytes 20 | tf_op jit(solution)/shard_map/ppermute | solution.py:62
  159.7 2.1 %collective-permute-done.9 = f32[]{:T(128)} collective-permute-done((f32[]{:T(128)}, f32[]{:T(128)}, u32[]{:S(2)}, u32[]{:S(2)}) %collective-permute-start.9) | collective-permute-done | bytes 36 | tf_op jit(solution)/shard_map/ppermute | solution.py:62
  163.1 5.8 %collective-permute-start.12 = (f32[]{:T(128)}, f32[]{:T(128)}, u32[]{:S(2)}, u32[]{:S(2)}) collective-permute-start(f32[]{:T(128)} %add.212), channel_id=1, source_target_pairs={{0,2},{1,3},{2,4},{3,5},{4,6},{5,7},{6,0},{7,1},{8,10},{9,11},{10,... | collective-permute-start | bytes 20 | tf_op jit(solution)/shard_map/ppermute | solution.py:62
  168.9 7.2 %collective-permute-start.11 = (f32[]{:T(128)}, f32[]{:T(128)}, u32[]{:S(2)}, u32[]{:S(2)}) collective-permute-start(f32[]{:T(128)} %add.212), channel_id=1, source_target_pairs={{0,4},{1,5},{2,6},{3,7},{4,0},{5,1},{6,2},{7,3},{8,12},{9,13},{10,... | collective-permute-start | bytes 20 | tf_op jit(solution)/shard_map/ppermute | solution.py:62
  176.1 6.5 %collective-permute-start.10 = (f32[]{:T(128)}, f32[]{:T(128)}, u32[]{:S(2)}, u32[]{:S(2)}) collective-permute-start(f32[]{:T(128)} %add.212), channel_id=1, source_target_pairs={{0,6},{1,7},{2,0},{3,1},{4,2},{5,3},{6,4},{7,5},{8,14},{9,15},{10,... | collective-permute-start | bytes 20 | tf_op jit(solution)/shard_map/ppermute | solution.py:62
  190.1 0.6 fusion
  190.7 5.2 %copy.56 = f32[16,64,8,64]{3,2,1,0:T(8,128)} copy(f32[16,64,8,64]{3,1,2,0:T(8,128)S(1)} %bitcast.28) | data formatting | bytes 4194304 | tf_op jit(solution)/shard_map/div | solution.py:146
  195.9 3.5 %div.94 = f32[1024,512]{1,0:T(8,128)S(1)} reshape(f32[16,64,8,64]{3,2,1,0:T(8,128)} %copy.56) | data formatting | bytes 4194304 | tf_op jit(solution)/shard_map/div | solution.py:146
  199.5 1.3 subtract_convert_fusion.1
  (30 shorter events, 1.3 us)
Async XLA Ops:
  8.3 7.1 %copy-start.1 = (bf16[1,1024,512]{2,1,0:T(8,128)(2,1)S(1)}, bf16[1,1024,512]{2,1,0:T(8,128)(2,1)}, u32[]{:S(2)}) copy-start(bf16[1,1024,512]{2,1,0:T(8,128)(2,1)} %param.8) | copy-start | bytes 3145732
  44.2 3.2 %collective-permute-start = (f32[258,64]{1,0:T(8,128)S(1)}, f32[258,64]{1,0:T(8,128)S(1)}, u32[]{:S(2)}, u32[]{:S(2)}) collective-permute-start(f32[258,64]{1,0:T(8,128)S(1)} %pad_maximum_fusion), channel_id=1, source_target_pairs={{0,8},{8,0},{16,24},{24,16},{32,40},{40,32},{48,56},{56,48},{64,72... | collective-permute-start | bytes 198152 | tf_op jit(solution)/shard_map/ppermute | solution.py:62
  47.5 13.0 %collective-permute-start.3 = (f32[258,64]{1,0:T(8,128)S(1)}, f32[258,64]{1,0:T(8,128)S(1)}, u32[]{:S(2)}, u32[]{:S(2)}) collective-permute-start(f32[258,64]{1,0:T(8,128)S(1)} %fusion.31), channel_id=1, source_target_pairs={{0,16},{8,24},{16,32},{24,40},{32,48},{40,56},{48,0},{56,8},{64,80... | collective-permute-start | bytes 198152 | tf_op jit(solution)/shard_map/ppermute | solution.py:62
  51.8 13.4 %collective-permute-start.2 = (f32[258,64]{1,0:T(8,128)S(1)}, f32[258,64]{1,0:T(8,128)S(1)}, u32[]{:S(2)}, u32[]{:S(2)}) collective-permute-start(f32[258,64]{1,0:T(8,128)S(1)} %fusion.31), channel_id=1, source_target_pairs={{0,32},{8,40},{16,48},{24,56},{32,0},{40,8},{48,16},{56,24},{64,96... | collective-permute-start | bytes 198152 | tf_op jit(solution)/shard_map/ppermute | solution.py:62
  57.9 9.7 %collective-permute-start.1 = (f32[258,64]{1,0:T(8,128)S(1)}, f32[258,64]{1,0:T(8,128)S(1)}, u32[]{:S(2)}, u32[]{:S(2)}) collective-permute-start(f32[258,64]{1,0:T(8,128)S(1)} %fusion.31), channel_id=1, source_target_pairs={{0,48},{8,56},{16,0},{24,8},{32,16},{40,24},{48,32},{56,40},{64,11... | collective-permute-start | bytes 198152 | tf_op jit(solution)/shard_map/ppermute | solution.py:62
  67.6 15.3 %collective-permute-start.5 = (f32[258,64]{1,0:T(8,128)S(1)}, f32[258,64]{1,0:T(8,128)S(1)}, u32[]{:S(2)}, u32[]{:S(2)}) collective-permute-start(f32[258,64]{1,0:T(8,128)S(1)} %select_add_fusion.2), channel_id=1, source_target_pairs={{0,64},{8,72},{16,80},{24,88},{32,96},{40,104},{48,112},{56,120},{... | collective-permute-start | bytes 198152 | tf_op jit(solution)/shard_map/ppermute | solution.py:62
  78.3 19.2 %collective-permute-start.4 = (f32[258,64]{1,0:T(8,128)S(1)}, f32[258,64]{1,0:T(8,128)S(1)}, u32[]{:S(2)}, u32[]{:S(2)}) collective-permute-start(f32[258,64]{1,0:T(8,128)S(1)} %select_add_fusion.2), channel_id=1, source_target_pairs={{0,128},{8,136},{16,144},{24,152},{32,160},{40,168},{48,176},{56,1... | collective-permute-start | bytes 198152 | tf_op jit(solution)/shard_map/ppermute | solution.py:62
  97.5 11.3 %collective-permute-start.8 = (f32[258,64]{1,0:T(8,128)S(1)}, f32[258,64]{1,0:T(8,128)S(1)}, u32[]{:S(2)}, u32[]{:S(2)}) collective-permute-start(f32[258,64]{1,0:T(8,128)S(1)} %select_add_fusion.1), channel_id=1, source_target_pairs={{0,192},{8,200},{16,208},{24,216},{32,224},{40,232},{48,240},{56,2... | collective-permute-start | bytes 198152 | tf_op jit(solution)/shard_map/ppermute | solution.py:62
  100.9 9.6 %collective-permute-start.7 = (f32[258,64]{1,0:T(8,128)S(1)}, f32[258,64]{1,0:T(8,128)S(1)}, u32[]{:S(2)}, u32[]{:S(2)}) collective-permute-start(f32[258,64]{1,0:T(8,128)S(1)} %select_add_fusion.1), channel_id=1, source_target_pairs={{0,384},{8,392},{16,400},{24,408},{32,416},{40,424},{48,432},{56,4... | collective-permute-start | bytes 198152 | tf_op jit(solution)/shard_map/ppermute | solution.py:62
  103.9 8.5 %collective-permute-start.6 = (f32[258,64]{1,0:T(8,128)S(1)}, f32[258,64]{1,0:T(8,128)S(1)}, u32[]{:S(2)}, u32[]{:S(2)}) collective-permute-start(f32[258,64]{1,0:T(8,128)S(1)} %select_add_fusion.1), channel_id=1, source_target_pairs={{0,576},{8,584},{16,592},{24,600},{32,608},{40,616},{48,624},{56,6... | collective-permute-start | bytes 198152 | tf_op jit(solution)/shard_map/ppermute | solution.py:62
  133.5 7.2 %copy-start = (f32[128,64,64]{0,2,1:T(8,128)S(1)}, f32[128,64,64]{0,2,1:T(8,128)}, u32[]{:S(2)}) copy-start(f32[128,64,64]{0,2,1:T(8,128)} %get-tuple-element.4) | copy-start | bytes 6291460
  156.3 5.5 %collective-permute-start.9 = (f32[]{:T(128)}, f32[]{:T(128)}, u32[]{:S(2)}, u32[]{:S(2)}) collective-permute-start(f32[]{:T(128)} %get-tuple-element.7), channel_id=1, source_target_pairs={{0,1},{1,0},{2,3},{3,2},{4,5},{5,4},{6,7},{7,6},{8,9},{9,8},{10,11... | collective-permute-start | bytes 20 | tf_op jit(solution)/shard_map/ppermute | solution.py:62
  163.1 19.5 %collective-permute-start.12 = (f32[]{:T(128)}, f32[]{:T(128)}, u32[]{:S(2)}, u32[]{:S(2)}) collective-permute-start(f32[]{:T(128)} %add.212), channel_id=1, source_target_pairs={{0,2},{1,3},{2,4},{3,5},{4,6},{5,7},{6,0},{7,1},{8,10},{9,11},{10,... | collective-permute-start | bytes 20 | tf_op jit(solution)/shard_map/ppermute | solution.py:62
  168.9 15.0 %collective-permute-start.11 = (f32[]{:T(128)}, f32[]{:T(128)}, u32[]{:S(2)}, u32[]{:S(2)}) collective-permute-start(f32[]{:T(128)} %add.212), channel_id=1, source_target_pairs={{0,4},{1,5},{2,6},{3,7},{4,0},{5,1},{6,2},{7,3},{8,12},{9,13},{10,... | collective-permute-start | bytes 20 | tf_op jit(solution)/shard_map/ppermute | solution.py:62
  176.1 9.0 %collective-permute-start.10 = (f32[]{:T(128)}, f32[]{:T(128)}, u32[]{:S(2)}, u32[]{:S(2)}) collective-permute-start(f32[]{:T(128)} %add.212), channel_id=1, source_target_pairs={{0,6},{1,7},{2,0},{3,1},{4,2},{5,3},{6,4},{7,5},{8,14},{9,15},{10,... | collective-permute-start | bytes 20 | tf_op jit(solution)/shard_map/ppermute | solution.py:62
  195.9 3.5 %copy-start.2 = (bf16[1024,512]{1,0:T(8,128)(2,1)S(1)}, bf16[1024,512]{1,0:T(8,128)(2,1)}, u32[]{:S(2)}) copy-start(bf16[1024,512]{1,0:T(8,128)(2,1)} %param.9) | copy-start | bytes 3145732
